TPU v7x, 256 devices: a whole 4x4x8 slice. The times are simulated.
256 devices in a mesh: graph: 8 (over z), index: 32 (over x, y, core).
Axes of the slice: x: 4, y: 4, z: 8, core: 2. Of those that a mesh axis runs over, the one named last changes fastest.
Arguments:
- features: bfloat16 [65536, 1024], P(('graph', 'index')), may hold values from -6 to 6
- q_weight: bfloat16 [1024, 1024], replicated, may hold values from -0.1875 to 0.1875
- q_bias: float32 [1024], replicated, may hold values from -3 to 3
- w_self: bfloat16 [1024, 1024], replicated, may hold values from -0.125 to 0.125
- w_neigh: bfloat16 [1024, 1024], replicated, may hold values from -0.125 to 0.125
- z_bias: float32 [1024], replicated, may hold values from -3 to 3
- centroids: bfloat16 [8192, 1024], P('index'), may hold values from -0.1875 to 0.1875
- requests: int32 [256, 32, 16], P(('graph', 'index')), may hold values from 0 to 255, as said below
- slots: int32 [65536, 50], P(('graph', 'index')), may hold values from 0 to 511
- importance: float32 [65536, 50], P(('graph', 'index')), may hold values from 0.1 to 10
- labels: int32 [65536, 1], P(('graph', 'index')), may hold values from 0 to 31; in each aligned block of 256 rows (0 to 255, 256 to 511, ...) at most 16 rows name the same one
Outputs:
- scores: bfloat16 [65536, 256], P(('graph', 'index'))
Inputs may be any that keep to these rules, and one draw needn't show every extreme that they name: `requests`: the 16 rows that a device asks of one device are distinct. `labels`: the rows of one device carry any one label at most 16 times.
All inputs are finite; a program needn't handle non-finite values.
Results may differ from a plain program's by a relative error of at most 0.0051.
Values may be sent and summed in bfloat16 or wider, within the bound.
No kernel may reach another device: no remote copies, remote signals or barrier semaphores. Data moves between devices by JAX's collectives and lax.ppermute only.
A program may use at most 64 MiB of HBM per device.

v0:
```python
import jax
import jax.numpy as jnp
from jax import lax
from jax.sharding import PartitionSpec as P


def place_rows(label_rows, peer_count, owner_slots):
    hits = (label_rows[:, None] == jnp.arange(peer_count, dtype=jnp.int32)[None, :]).astype(
        jnp.int32
    )
    ranks = jnp.sum(hits * (jnp.cumsum(hits, axis=0) - 1), axis=1)
    return label_rows * owner_slots + ranks


def body(
    features,
    q_weight,
    q_bias,
    w_self,
    w_neigh,
    z_bias,
    centroids,
    requests,
    slots,
    importance,
    labels,
):
    row_count = features.shape[0]
    width = features.shape[1]
    peer_count = lax.axis_size("index")
    owner_slots = max(2 * row_count // peer_count, 2)
    fetch_slots = requests.shape[2]
    slot_count = peer_count * fetch_slots
    cent_count = centroids.shape[0]
    messages = jax.nn.relu(
        jnp.dot(features, q_weight, preferred_element_type=jnp.float32) + q_bias
    ).astype(jnp.bfloat16)
    weights_norm = importance / jnp.sum(importance, axis=1, keepdims=True)
    slot_ids = jnp.arange(slot_count, dtype=jnp.int32)
    mixing = jnp.sum(
        jnp.where(slots[:, :, None] == slot_ids[None, None, :], weights_norm[:, :, None], 0.0),
        axis=1,
    ).astype(jnp.bfloat16)
    asked_rows = requests[0]
    columns = (jnp.arange(peer_count, dtype=jnp.int32)[:, None] * row_count + asked_rows).reshape(
        -1
    )
    shard_rows = lax.all_gather(messages, "index", axis=0, tiled=True)
    targets = jnp.arange(shard_rows.shape[0], dtype=jnp.int32)
    select = (columns[:, None] == targets[None, :]).astype(jnp.bfloat16)
    local_mix = jnp.dot(mixing, select, preferred_element_type=jnp.float32).astype(jnp.bfloat16)
    pooled = jnp.dot(local_mix, shard_rows, preferred_element_type=jnp.float32).astype(jnp.bfloat16)
    hidden = jax.nn.relu(
        jnp.dot(features, w_self, preferred_element_type=jnp.float32)
        + jnp.dot(pooled, w_neigh, preferred_element_type=jnp.float32)
        + z_bias
    )
    normed = (hidden * lax.rsqrt(jnp.mean(hidden * hidden, axis=1, keepdims=True) + 1e-06)).astype(
        jnp.bfloat16
    )
    positions = place_rows(labels[:, 0], peer_count, owner_slots)
    outgoing = jnp.zeros((peer_count * owner_slots, width), jnp.bfloat16).at[positions].set(normed)
    outgoing = outgoing.reshape(peer_count, owner_slots, width)
    arrived = lax.all_to_all(outgoing, "index", split_axis=0, concat_axis=0, tiled=True)
    flat_rows = arrived.reshape(-1, width)
    raw_scores = lax.dot_general(
        flat_rows, centroids, (((1,), (1,)), ((), ())), preferred_element_type=jnp.float32
    ).astype(jnp.bfloat16)
    returned = lax.all_to_all(
        raw_scores.reshape(peer_count, arrived.shape[1], cent_count),
        "index",
        split_axis=0,
        concat_axis=0,
        tiled=True,
    )
    return jnp.take(returned.reshape(peer_count * owner_slots, cent_count), positions, axis=0)


def solution(mesh):
    return jax.shard_map(
        body,
        mesh=mesh,
        in_specs=(
            P(("graph", "index"), None),
            P(),
            P(),
            P(),
            P(),
            P(),
            P("index", None),
            P(("graph", "index"), None, None),
            P(("graph", "index"), None),
            P(("graph", "index"), None),
            P(("graph", "index"), None),
        ),
        out_specs=P(("graph", "index"), None),
        check_vma=False,
    )
```

profile of v0, /device:TPU:1, one launch (start us, length us, event | category | flops | bytes accessed | tf_op | source)
XLA Modules:
  0.0 157.9 jit_solution(2172028200246087104)
XLA Ops:
  6.5 0.0 copy-start
  6.5 0.0 copy-start.4
  6.5 0.0 copy-start.5
  6.5 0.0 all-gather.2.cloned.1.call-start
  6.6 3.3 %fusion.6 = bf16[256,1024]{1,0:T(8,128)(2,1)} fusion(bf16[256,1024]{1,0:T(8,128)(2,1)} %param.11, bf16[1024,1024]{1,0:T(8,128)(2,1)} %param.12, f32[1024]{0:T(1024)} %param.13), kind=kOutput, calls=%fused_computation.13 | convolution fusion | flops 537657344 | bytes 3149824 | tf_op jit(solution)/shard_map/dot_general | solution.py:36
  9.9 0.0 all-gather.2.cloned.1.call-update
  9.9 0.0 copy-done.4
  10.0 0.6 reduce-window.6
  10.6 0.2 slice_reduce_fusion
  10.8 0.1 add.67
  10.9 0.1 add.68
  10.9 0.0 copy-done.5
  11.0 0.1 copy.19
  11.0 0.1 squeeze.4
  11.1 0.0 copy-done.1
  11.2 0.1 fusion.13
  11.3 2.5 %fusion.15 = f32[256,1024]{1,0:T(8,128)S(1)} fusion(bf16[256,1024]{1,0:T(8,128)(2,1)} %param.11, bf16[1024,1024]{1,0:T(8,128)(2,1)} %param.14), kind=kOutput, calls=%fused_computation.37 | convolution fusion | flops 536870912 | bytes 3670016 | tf_op jit(solution)/shard_map/dot_general | solution.py:54
  13.8 0.0 copy-done.2
  13.8 4.3 %select_reduce_fusion = bf16[256,512]{1,0:T(8,128)(2,1)S(1)} fusion(f32[256,50]{0,1:T(8,128)S(1)} %broadcast_divide_fusion, s32[256,50]{0,1:T(8,128)S(1)} %copy-done.2), kind=kLoop, calls=%fused_computation.2 | loop fusion | flops 19529728 | bytes 364544 | tf_op jit(solution)/shard_map/reduce_sum | solution.py:40
  18.1 0.0 copy-start.3
  18.2 73.7 %all-gather.2.cloned.1.call-done = bf16[8192,1024]{1,0:T(8,128)(2,1)} async-done(((bf16[256,1024]{1,0:T(8,128)(2,1)}), bf16[8192,1024]{1,0:T(8,128)(2,1)}) %all-gather.2.cloned.1.call-update) | async-done | bytes 16777232 | tf_op jit(solution)/shard_map/all_gather | solution.py:48
  91.8 14.6 %convolution_convert_fusion = bf16[256,1024]{1,0:T(8,128)(2,1)} fusion(bf16[8192,1024]{1,0:T(8,128)(2,1)} %all-gather.2.cloned.1.call-done, s32[512]{0:T(512)S(1)} %add.69, bf16[256,512]{1,0:T(8,128)(2,1)S(1)} %select_reduce_fusion), kind=kOutput, calls=%fused_computation.14 | convolution fusion | flops 6449004544 | bytes 17565696 | tf_op jit(solution)/shard_map/dot_general | solution.py:52
  106.4 0.0 copy-done
  106.4 0.0 copy-done.3
  106.4 2.8 %multiply_reduce_fusion = (f32[256]{0:T(256)S(1)}, f32[256,1024]{1,0:T(8,128)}) fusion(f32[1024]{0:T(1024)S(1)} %copy-done.3, f32[256,1024]{1,0:T(8,128)S(1)} %fusion.15, bf16[256,1024]{1,0:T(8,128)(2,1)} %convolution_convert_fusion, bf16[1024,1024]{1,0:T(8,128)(2,1)S(1)} %copy-done), kind=kOutput, calls=%fused_computation.17 | convolution fusion | flops 538181376 | bytes 4723712 | tf_op jit(solution)/shard_map/dot_general | solution.py:55
  109.2 2.7 %scatter_custom_fusion = bf16[512,1024]{1,0:T(8,128)(2,1)S(1)} fusion(s32[256]{0:T(256)S(1)} %bitcast.38, f32[256,1024]{1,0:T(8,128)} %get-tuple-element.8, f32[256]{0:T(256)S(1)} %add_rsqrt_fusion, bf16[]{:T(256)} %constant.36.clone.1), kind=kCustom, calls=%fused_computation.18 | custom fusion | flops 524288 | bytes 2098178 | tf_op jit(solution)/shard_map/scatter | solution.py:62
  111.9 22.1 %all_to_all.10 = bf16[32,16,1024]{2,1,0:T(8,128)(2,1)S(1)} all-to-all(bf16[32,16,1024]{2,1,0:T(8,128)(2,1)S(1)} %bitcast.34), channel_id=1, replica_groups=mesh['graph'=8,'index'=32] {'index'}, dimensions={0} | all-to-all | bytes 2097152 | tf_op jit(solution)/shard_map/all_to_all | solution.py:64
  134.0 2.2 %convolution_convert_fusion.1 = bf16[512,256]{1,0:T(8,128)(2,1)} fusion(bf16[512,1024]{1,0:T(8,128)(2,1)S(1)} %bitcast.35, bf16[256,1024]{1,0:T(8,128)(2,1)} %param.17), kind=kOutput, calls=%fused_computation.15 | convolution fusion | flops 268566528 | bytes 1835008 | tf_op jit(solution)/shard_map/dot_general | solution.py:66
  136.2 3.9 %all-to-all-start.1 = ((bf16[32,16,256]{2,1,0:T(8,128)(2,1)}), bf16[32,16,256]{2,1,0:T(8,128)(2,1)S(1)}, u32[]{:S(2)}, u32[]{:S(2)}) async-start(bf16[32,16,256]{2,1,0:T(8,128)(2,1)} %bitcast.7), calls=%async_computation.1 | async-start | bytes 524288 | tf_op jit(solution)/shard_map/all_to_all | solution.py:69
  140.2 8.9 %all-to-all-done.1 = bf16[32,16,256]{2,1,0:T(8,128)(2,1)S(1)} async-done(((bf16[32,16,256]{2,1,0:T(8,128)(2,1)}), bf16[32,16,256]{2,1,0:T(8,128)(2,1)S(1)}, u32[]{:S(2)}, u32[]{:S(2)}) %all-to-all-start.1) | async-done | bytes 262176 | tf_op jit(solution)/shard_map/all_to_all | solution.py:69
  149.1 1.2 gather_fusion
  150.2 0.8 broadcast_select_fusion
  (12 shorter events, 0.1 us)
Async XLA Ops:
  6.5 99.9 %copy-start = (bf16[1024,1024]{1,0:T(8,128)(2,1)S(1)}, bf16[1024,1024]{1,0:T(8,128)(2,1)}, u32[]{:S(2)}) copy-start(bf16[1024,1024]{1,0:T(8,128)(2,1)} %param.15) | copy-start | bytes 6291460
  6.5 3.4 %copy-start.4 = (s32[256,1]{0,1:T(1,128)S(1)}, s32[256,1]{0,1:T(1,128)}, u32[]{:S(2)}) copy-start(s32[256,1]{0,1:T(1,128)} %param.21) | copy-start | bytes 3076
  6.5 4.4 %copy-start.5 = (s32[1,32,16]{1,2,0:T(8,128)S(1)}, s32[1,32,16]{1,2,0:T(8,128)}, u32[]{:S(2)}) copy-start(s32[1,32,16]{1,2,0:T(8,128)} %param.18) | copy-start | bytes 6148
  6.5 4.6 %copy-start.1 = (f32[256,50]{0,1:T(8,128)S(1)}, f32[256,50]{0,1:T(8,128)}, u32[]{:S(2)}) copy-start(f32[256,50]{0,1:T(8,128)} %param.20) | copy-start | bytes 153604
  6.5 7.2 %copy-start.2 = (s32[256,50]{0,1:T(8,128)S(1)}, s32[256,50]{0,1:T(8,128)}, u32[]{:S(2)}) copy-start(s32[256,50]{0,1:T(8,128)} %param.19) | copy-start | bytes 153604
  6.5 85.3 %all-gather.2.cloned.1.call-start = ((), (), s32[]{:S(2)}) async-start(), calls=%async_computation.2 | async-start | bytes 17301504 | tf_op jit(solution)/shard_map/all_gather | solution.py:48
  18.1 88.3 %copy-start.3 = (f32[1024]{0:T(1024)S(1)}, f32[1024]{0:T(1024)}, u32[]{:S(2)}) copy-start(f32[1024]{0:T(1024)} %param.16) | copy-start | bytes 12292
  136.2 12.9 %all-to-all-start.1 = ((bf16[32,16,256]{2,1,0:T(8,128)(2,1)}), bf16[32,16,256]{2,1,0:T(8,128)(2,1)S(1)}, u32[]{:S(2)}, u32[]{:S(2)}) async-start(bf16[32,16,256]{2,1,0:T(8,128)(2,1)} %bitcast.7), calls=%async_computation.1 | async-start | bytes 524288 | tf_op jit(solution)/shard_map/all_to_all | solution.py:69
Sparse Core Ops, SparseCore 0:
  10.1 81.7 all-gather.1
where the time goes:
time: 158 us
  waiting for transfers between devices  82.6 us (52%)
  matrix products  25.4 us (16%)
  blocking collectives  22.1 us (14%)
  between operations  13.5 us (9%)
  other arithmetic  8.59 us (5%)
  starting transfers between devices  3.96 us (3%)
  local copies, waits for them, and re-layouts  1.68 us (1%)
    all_gather x1, waiting for transfers between devices, body(): shard_rows = lax.all_gather(messages, 'index', axis=0, tiled=True)  73.7 us
    all_to_all x1, blocking collectives, body(): lax.all_to_all(outgoing, 'index', split_axis=0, concat_axis=0, tiled=True)  22.1 us
    dot_general x1, matrix products, body(): jnp.dot(local_mix, shard_rows, preferred_element_type=jnp.float32)  14.6 us
    all_to_all x1, waiting for transfers between devices, body(): lax.all_to_all(raw_scores.reshape(peer_count, arrived.shape[1], cent_coun...  8.95 us
    reduce_sum x1, other arithmetic, body(): jnp.sum(jnp.where(slots[:, :, None] == slot_ids[None, None, :], weights_n...  4.35 us
    all_to_all x1, starting transfers between devices, body(): lax.all_to_all(raw_scores.reshape(peer_count, arrived.shape[1], cent_coun...  3.92 us
    dot_general x1, matrix products, body(): jnp.dot(features, q_weight, preferred_element_type=jnp.float32) + q_bias  3.32 us
  transfers between devices with their start and end apart: 2, of which 2 were waited for; matrix products, arithmetic and copies ran while one was open for 5% of the time, Pallas kernels for 0%

commit v1 on v0

--- a/solution.py
+++ b/solution.py
@@ -42,14 +42,16 @@
         axis=1,
     ).astype(jnp.bfloat16)
     asked_rows = requests[0]
-    columns = (jnp.arange(peer_count, dtype=jnp.int32)[:, None] * row_count + asked_rows).reshape(
-        -1
-    )
-    shard_rows = lax.all_gather(messages, "index", axis=0, tiled=True)
-    targets = jnp.arange(shard_rows.shape[0], dtype=jnp.int32)
-    select = (columns[:, None] == targets[None, :]).astype(jnp.bfloat16)
-    local_mix = jnp.dot(mixing, select, preferred_element_type=jnp.float32).astype(jnp.bfloat16)
-    pooled = jnp.dot(local_mix, shard_rows, preferred_element_type=jnp.float32).astype(jnp.bfloat16)
+    wanted = lax.all_to_all(asked_rows, "index", split_axis=0, concat_axis=0, tiled=True)
+    outgoing_msgs = jnp.take(messages, wanted.reshape(-1), axis=0)
+    fetched = lax.all_to_all(
+        outgoing_msgs.reshape(peer_count, fetch_slots, width),
+        "index",
+        split_axis=0,
+        concat_axis=0,
+        tiled=True,
+    ).reshape(slot_count, width)
+    pooled = jnp.dot(mixing, fetched, preferred_element_type=jnp.float32).astype(jnp.bfloat16)
     hidden = jax.nn.relu(
         jnp.dot(features, w_self, preferred_element_type=jnp.float32)
         + jnp.dot(pooled, w_neigh, preferred_element_type=jnp.float32)

time: 158 us -> 90.2 us (0.57)
  waiting for transfers between devices: 82.6 us -> 22.4 us
  matrix products: 25.4 us -> 8.72 us
  starting transfers between devices: 3.96 us -> 19 us
  between operations: 13.5 us -> 0.15 us
  local copies, waits for them, and re-layouts: 1.68 us -> 6.29 us
  other arithmetic: 8.59 us -> 12.4 us
    all_gather x1 -> x0, waiting for transfers between devices: 73.7 us -> none  [body(): shard_rows = lax.all_gather(messages, 'index', axis=0, tiled=True)]
    all_to_all x0 -> x2, starting transfers between devices: none -> 15.1 us  [the longest x1 8.58 us: body(): lax.all_to_all(asked_rows, 'index', split_axis=0, concat_axis=0, tiled=True)]
    dot_general x1 -> x0, matrix products: 14.6 us -> none  [body(): jnp.dot(local_mix, shard_rows, preferred_element_type=jnp.float32)]
    all_to_all x0 -> x2, waiting for transfers between devices: none -> 13.5 us  [the longest x1 12.5 us: body(): lax.all_to_all(outgoing_msgs.reshape(peer_count, fetch_slots, width), 'in...]
    gather x0 -> x1, local copies, waits for them, and re-layouts: none -> 2.79 us  [body(): outgoing_msgs = jnp.take(messages, wanted.reshape(-1), axis=0)]
    dot_general x1, matrix products: 3.32 us -> 0.71 us  [body(): jnp.dot(features, q_weight, preferred_element_type=jnp.float32) + q_bias]
    select_n x0 -> x2, other arithmetic: none -> 2.47 us  [body(): outgoing_msgs = jnp.take(messages, wanted.reshape(-1), axis=0)]
  transfers between devices with their start and end apart: 2 -> 3, of which waited for: 2 -> 3; matrix products, arithmetic and copies ran while one was open for 5% -> 11% of each run, Pallas kernels for 0% -> 0%
where the time goes in v1:
time: 90.2 us; the launch traced here: 89.7 us
  waiting for transfers between devices  22.4 us (25%)
  blocking collectives  20.8 us (23%)
  starting transfers between devices  19 us (21%)
  other arithmetic  12.4 us (14%)
  matrix products  8.72 us (10%)
  local copies, waits for them, and re-layouts  6.29 us (7%)
    all_to_all x1, blocking collectives, body(): lax.all_to_all(outgoing, 'index', split_axis=0, concat_axis=0, tiled=True)  20.8 us
    all_to_all x1, waiting for transfers between devices, body(): lax.all_to_all(outgoing_msgs.reshape(peer_count, fetch_slots, width), 'in...  12.5 us
    all_to_all x1, waiting for transfers between devices, body(): lax.all_to_all(raw_scores.reshape(peer_count, arrived.shape[1], cent_coun...  8.95 us
    all_to_all x1, starting transfers between devices, body(): lax.all_to_all(asked_rows, 'index', split_axis=0, concat_axis=0, tiled=True)  8.58 us
    all_to_all x1, starting transfers between devices, body(): lax.all_to_all(outgoing_msgs.reshape(peer_count, fetch_slots, width), 'in...  6.49 us
    reduce_sum x1, other arithmetic, body(): jnp.sum(jnp.where(slots[:, :, None] == slot_ids[None, None, :], weights_n...  4.35 us
    all_to_all x1, starting transfers between devices, body(): lax.all_to_all(raw_scores.reshape(peer_count, arrived.shape[1], cent_coun...  3.93 us
    dot_general x1, matrix products, body(): jnp.dot(features, w_self, preferred_element_type=jnp.float32)  3.61 us
  transfers between devices with their start and end apart: 3, of which 3 were waited for; matrix products, arithmetic and copies ran while one was open for 11% of the time, Pallas kernels for 0%

profile of v1, /device:TPU:1, one launch (start us, length us, event | category | flops | bytes accessed | tf_op | source)
XLA Modules:
  0.0 89.7 jit_solution(7447523668793121859)
XLA Ops:
  0.0 0.0 copy-start
  0.0 1.5 %copy.25 = s32[1,32,16]{2,1,0:T(8,128)} copy(s32[1,32,16]{1,2,0:T(8,128)} %param.18) | data formatting | bytes 4096 | tf_op args[7]
  1.5 8.6 %all-to-all-start = ((s32[32,1,16]{2,1,0:T(1,128)}), s32[32,1,16]{2,1,0:T(1,128)S(1)}, u32[]{:S(2)}, u32[]{:S(2)}) async-start(s32[32,1,16]{2,1,0:T(1,128)} %bitcast.5), calls=%async_computation | async-start | bytes 32768 | tf_op jit(solution)/shard_map/all_to_all | solution.py:45
  10.1 0.7 fusion.11
  10.8 0.6 reduce-window.6
  11.4 0.2 slice_reduce_fusion
  11.6 3.6 %fusion.12 = f32[256,1024]{1,0:T(8,128)} fusion(bf16[256,1024]{1,0:T(8,128)(2,1)} %param.11, bf16[1024,1024]{1,0:T(8,128)(2,1)} %param.14), kind=kOutput, calls=%fused_computation.38 | convolution fusion | flops 536870912 | bytes 3670016 | tf_op jit(solution)/shard_map/dot_general | solution.py:56
  15.2 0.0 copy-done.2
  15.2 0.0 copy-done.8
  15.2 0.0 copy-start.5
  15.2 0.7 fusion.3
  16.0 0.1 fusion.10
  16.1 1.0 %all-to-all-done = s32[32,1,16]{2,1,0:T(1,128)S(1)} async-done(((s32[32,1,16]{2,1,0:T(1,128)}), s32[32,1,16]{2,1,0:T(1,128)S(1)}, u32[]{:S(2)}, u32[]{:S(2)}) %all-to-all-start) | async-done | bytes 2080 | tf_op jit(solution)/shard_map/all_to_all | solution.py:45
  17.0 0.5 broadcast.97
  17.5 0.7 reduce.7
  18.2 0.1 reshape.105
  18.3 2.8 %gather_fusion = bf16[512,1024]{1,0:T(8,128)(2,1)} fusion(bf16[256,1024]{1,0:T(8,128)(2,1)S(1)} %fusion.3, s32[1024]{0:T(1024)S(1)} %pad_clamp_fusion.1), kind=kCustom, calls=%fused_computation | custom fusion | bytes 2099200 | tf_op jit(solution)/shard_map/jit(_take)/gather | solution.py:46
  21.1 2.5 %broadcast_select_fusion = bf16[32,16,1024]{2,1,0:T(8,128)(2,1)} fusion(bf16[32,16,1024]{2,1,0:T(8,128)(2,1)} %bitcast.39, pred[32,16]{1,0:T(8,128)(4,1)S(1)} %compare_and_fusion), kind=kLoop, calls=%fused_computation.15 | loop fusion | flops 524288 | bytes 2097664 | tf_op jit(solution)/shard_map/jit(_take)/select_n | solution.py:46
  23.6 6.5 %all-to-all-start.1 = ((bf16[32,16,1024]{2,1,0:T(8,128)(2,1)}), bf16[32,16,1024]{2,1,0:T(8,128)(2,1)}, u32[]{:S(2)}, u32[]{:S(2)}) async-start(bf16[32,16,1024]{2,1,0:T(8,128)(2,1)} %broadcast_select_fusion), calls=%async_computation.1 | async-start | bytes 2097152 | tf_op jit(solution)/shard_map/all_to_all | solution.py:47
  30.1 0.0 copy-done.3
  30.2 4.3 %select_reduce_fusion = bf16[256,512]{1,0:T(8,128)(2,1)S(1)} fusion(f32[256,50]{0,1:T(8,128)S(1)} %broadcast_divide_fusion, s32[256,50]{0,1:T(8,128)S(1)} %copy-done.4), kind=kLoop, calls=%fused_computation.3 | loop fusion | flops 19529728 | bytes 364544 | tf_op jit(solution)/shard_map/reduce_sum | solution.py:40
  34.6 12.5 %all-to-all-done.1 = bf16[32,16,1024]{2,1,0:T(8,128)(2,1)} async-done(((bf16[32,16,1024]{2,1,0:T(8,128)(2,1)}), bf16[32,16,1024]{2,1,0:T(8,128)(2,1)}, u32[]{:S(2)}, u32[]{:S(2)}) %all-to-all-start.1) | async-done | bytes 1048608 | tf_op jit(solution)/shard_map/all_to_all | solution.py:47
  47.1 3.2 %multiply_reduce_fusion = (f32[256]{0:T(256)S(1)}, f32[256,1024]{1,0:T(8,128)}) fusion(f32[1024]{0:T(1024)S(1)} %copy-done.9, f32[256,1024]{1,0:T(8,128)S(1)} %copy-done.1, bf16[1024,1024]{1,0:T(8,128)(2,1)S(1)} %copy-done, bf16[512,1024]{1,0:T(8,128)(2,1)} %bitcast.9, bf16[256,512]{1,0:T(8,128)(2,1)S(1)} %select_reduce_fusion), kind=kOutput, calls=%fused_computation.14 | convolution fusion | flops 806878976 | bytes 5510144 | tf_op jit(solution)/shard_map/dot_general | solution.py:57
  50.3 2.7 %scatter_custom_fusion = bf16[512,1024]{1,0:T(8,128)(2,1)S(1)} fusion(s32[256]{0:T(256)S(1)} %bitcast.46, f32[256,1024]{1,0:T(8,128)} %get-tuple-element.8, f32[256]{0:T(256)S(1)} %add_rsqrt_fusion, bf16[]{:T(256)} %constant.47.clone.1), kind=kCustom, calls=%fused_computation.16 | custom fusion | flops 524288 | bytes 2098178 | tf_op jit(solution)/shard_map/scatter | solution.py:64
  53.0 0.0 copy-start.7
  53.0 20.8 %all_to_all.24 = bf16[32,16,1024]{2,1,0:T(8,128)(2,1)S(1)} all-to-all(bf16[32,16,1024]{2,1,0:T(8,128)(2,1)S(1)} %bitcast.40), channel_id=1, replica_groups=mesh['graph'=8,'index'=32] {'index'}, dimensions={0} | all-to-all | bytes 2097152 | tf_op jit(solution)/shard_map/all_to_all | solution.py:66
  73.8 0.0 copy-done.7
  73.8 1.2 %convolution_convert_fusion.1 = bf16[512,256]{1,0:T(8,128)(2,1)} fusion(bf16[512,1024]{1,0:T(8,128)(2,1)S(1)} %bitcast.41, bf16[256,1024]{1,0:T(8,128)(2,1)S(1)} %copy-done.7), kind=kOutput, calls=%fused_computation.12 | convolution fusion | flops 268566528 | bytes 1835008 | tf_op jit(solution)/shard_map/dot_general | solution.py:68
  74.9 3.9 %all-to-all-start.3 = ((bf16[32,16,256]{2,1,0:T(8,128)(2,1)}), bf16[32,16,256]{2,1,0:T(8,128)(2,1)S(1)}, u32[]{:S(2)}, u32[]{:S(2)}) async-start(bf16[32,16,256]{2,1,0:T(8,128)(2,1)} %bitcast.12), calls=%async_computation.3 | async-start | bytes 524288 | tf_op jit(solution)/shard_map/all_to_all | solution.py:71
  78.9 8.9 %all-to-all-done.3 = bf16[32,16,256]{2,1,0:T(8,128)(2,1)S(1)} async-done(((bf16[32,16,256]{2,1,0:T(8,128)(2,1)}), bf16[32,16,256]{2,1,0:T(8,128)(2,1)S(1)}, u32[]{:S(2)}, u32[]{:S(2)}) %all-to-all-start.3) | async-done | bytes 262176 | tf_op jit(solution)/shard_map/all_to_all | solution.py:71
  87.8 1.2 %gather_fusion.1 = bf16[256,256]{1,0:T(8,128)(2,1)S(1)} fusion(bf16[512,256]{1,0:T(8,128)(2,1)S(1)} %bitcast.38, s32[1024]{0:T(1024)S(1)} %pad_clamp_fusion), kind=kCustom, calls=%fused_computation.1 | custom fusion | bytes 263168 | tf_op jit(solution)/shard_map/jit(_take)/gather | solution.py:78
  89.0 0.8 broadcast_select_fusion.1
  (23 shorter events, 0.2 us)
Async XLA Ops:
  0.0 47.1 %copy-start = (bf16[1024,1024]{1,0:T(8,128)(2,1)S(1)}, bf16[1024,1024]{1,0:T(8,128)(2,1)}, u32[]{:S(2)}) copy-start(bf16[1024,1024]{1,0:T(8,128)(2,1)} %param.15) | copy-start | bytes 6291460
  0.0 15.2 %copy-start.2 = (bf16[256,1024]{1,0:T(8,128)(2,1)S(1)}, bf16[256,1024]{1,0:T(8,128)(2,1)}, u32[]{:S(2)}) copy-start(bf16[256,1024]{1,0:T(8,128)(2,1)} %param.11) | copy-start | bytes 1572868
  0.0 15.2 %copy-start.8 = (f32[1024]{0:T(1024)S(1)}, f32[1024]{0:T(1024)}, u32[]{:S(2)}) copy-start(f32[1024]{0:T(1024)} %param.13) | copy-start | bytes 12292
  1.5 15.5 %all-to-all-start = ((s32[32,1,16]{2,1,0:T(1,128)}), s32[32,1,16]{2,1,0:T(1,128)S(1)}, u32[]{:S(2)}, u32[]{:S(2)}) async-start(s32[32,1,16]{2,1,0:T(1,128)} %bitcast.5), calls=%async_computation | async-start | bytes 32768 | tf_op jit(solution)/shard_map/all_to_all | solution.py:45
  11.6 3.6 %copy-start.6 = (bf16[1024,1024]{1,0:T(8,128)(2,1)S(1)}, bf16[1024,1024]{1,0:T(8,128)(2,1)}, u32[]{:S(2)}) copy-start(bf16[1024,1024]{1,0:T(8,128)(2,1)} %param.12) | copy-start | bytes 6291460
  15.2 0.7 copy-start.5
  21.1 9.0 %copy-start.3 = (f32[256,50]{0,1:T(8,128)S(1)}, f32[256,50]{0,1:T(8,128)}, u32[]{:S(2)}) copy-start(f32[256,50]{0,1:T(8,128)} %param.20) | copy-start | bytes 153604
  21.1 9.1 %copy-start.4 = (s32[256,50]{0,1:T(8,128)S(1)}, s32[256,50]{0,1:T(8,128)}, u32[]{:S(2)}) copy-start(s32[256,50]{0,1:T(8,128)} %param.19) | copy-start | bytes 153604
  21.1 25.9 %copy-start.1 = (f32[256,1024]{1,0:T(8,128)S(1)}, f32[256,1024]{1,0:T(8,128)}, u32[]{:S(2)}) copy-start(f32[256,1024]{1,0:T(8,128)} %fusion.12) | copy-start | bytes 3145732
  21.1 25.9 %copy-start.9 = (f32[1024]{0:T(1024)S(1)}, f32[1024]{0:T(1024)}, u32[]{:S(2)}) copy-start(f32[1024]{0:T(1024)} %param.16) | copy-start | bytes 12292
  23.6 23.5 %all-to-all-start.1 = ((bf16[32,16,1024]{2,1,0:T(8,128)(2,1)}), bf16[32,16,1024]{2,1,0:T(8,128)(2,1)}, u32[]{:S(2)}, u32[]{:S(2)}) async-start(bf16[32,16,1024]{2,1,0:T(8,128)(2,1)} %broadcast_select_fusion), calls=%async_computation.1 | async-start | bytes 2097152 | tf_op jit(solution)/shard_map/all_to_all | solution.py:47
  53.0 20.8 %copy-start.7 = (bf16[256,1024]{1,0:T(8,128)(2,1)S(1)}, bf16[256,1024]{1,0:T(8,128)(2,1)}, u32[]{:S(2)}) copy-start(bf16[256,1024]{1,0:T(8,128)(2,1)} %param.17) | copy-start | bytes 1572868
  74.9 12.9 %all-to-all-start.3 = ((bf16[32,16,256]{2,1,0:T(8,128)(2,1)}), bf16[32,16,256]{2,1,0:T(8,128)(2,1)S(1)}, u32[]{:S(2)}, u32[]{:S(2)}) async-start(bf16[32,16,256]{2,1,0:T(8,128)(2,1)} %bitcast.12), calls=%async_computation.3 | async-start | bytes 524288 | tf_op jit(solution)/shard_map/all_to_all | solution.py:71

commit v2 on v1

--- a/solution.py
+++ b/solution.py
@@ -10,6 +10,10 @@
     )
     ranks = jnp.sum(hits * (jnp.cumsum(hits, axis=0) - 1), axis=1)
     return label_rows * owner_slots + ranks
+
+
+def one_hot(index, count):
+    return (index[:, None] == jnp.arange(count, dtype=jnp.int32)[None, :]).astype(jnp.bfloat16)
 
 
 def body(
@@ -32,6 +36,8 @@
     fetch_slots = requests.shape[2]
     slot_count = peer_count * fetch_slots
     cent_count = centroids.shape[0]
+    me = lax.axis_index("index")
+    all_requests = lax.all_gather(requests[0], "index", axis=0, tiled=False)
     messages = jax.nn.relu(
         jnp.dot(features, q_weight, preferred_element_type=jnp.float32) + q_bias
     ).astype(jnp.bfloat16)
@@ -41,9 +47,10 @@
         jnp.where(slots[:, :, None] == slot_ids[None, None, :], weights_norm[:, :, None], 0.0),
         axis=1,
     ).astype(jnp.bfloat16)
-    asked_rows = requests[0]
-    wanted = lax.all_to_all(asked_rows, "index", split_axis=0, concat_axis=0, tiled=True)
-    outgoing_msgs = jnp.take(messages, wanted.reshape(-1), axis=0)
+    wanted = lax.dynamic_index_in_dim(all_requests, me, axis=1, keepdims=False)
+    outgoing_msgs = jnp.dot(
+        one_hot(wanted.reshape(-1), row_count), messages, preferred_element_type=jnp.float32
+    ).astype(jnp.bfloat16)
     fetched = lax.all_to_all(
         outgoing_msgs.reshape(peer_count, fetch_slots, width),
         "index",
@@ -61,7 +68,10 @@
         jnp.bfloat16
     )
     positions = place_rows(labels[:, 0], peer_count, owner_slots)
-    outgoing = jnp.zeros((peer_count * owner_slots, width), jnp.bfloat16).at[positions].set(normed)
+    pick = one_hot(positions, peer_count * owner_slots)
+    outgoing = lax.dot_general(
+        pick, normed, (((0,), (0,)), ((), ())), preferred_element_type=jnp.float32
+    ).astype(jnp.bfloat16)
     outgoing = outgoing.reshape(peer_count, owner_slots, width)
     arrived = lax.all_to_all(outgoing, "index", split_axis=0, concat_axis=0, tiled=True)
     flat_rows = arrived.reshape(-1, width)
@@ -75,7 +85,10 @@
         concat_axis=0,
         tiled=True,
     )
-    return jnp.take(returned.reshape(peer_count * owner_slots, cent_count), positions, axis=0)
+    return jnp.dot(
+        pick, returned.reshape(peer_count * owner_slots, cent_count),
+        preferred_element_type=jnp.float32,
+    ).astype(jnp.bfloat16)
 
 
 def solution(mesh):

time: 90.2 us -> 93.7 us (1.039)
  blocking collectives: 20.8 us -> 59.9 us
  starting transfers between devices: 19 us -> 5.29 us
  waiting for transfers between devices: 22.4 us -> 9.06 us
  other arithmetic: 12.4 us -> 5.13 us
  local copies, waits for them, and re-layouts: 6.29 us -> 1.01 us
  matrix products: 8.72 us -> 12.8 us
    all_gather x0 -> x1, blocking collectives: none -> 26.6 us  [body(): all_requests = lax.all_gather(requests[0], 'index', axis=0, tiled=False)]
    all_to_all x0 -> x1, blocking collectives: none -> 12.7 us  [body(): lax.all_to_all(raw_scores.reshape(peer_count, arrived.shape[1], cent_coun...]
    all_to_all x2 -> x0, starting transfers between devices: 12.5 us -> none  [the longest x1 8.58 us: body(): lax.all_to_all(asked_rows, 'index', split_axis=0, concat_axis=0, tiled=True)]
    all_to_all x2 -> x0, waiting for transfers between devices: 9.9 us -> none  [the longest x1 8.95 us: body(): lax.all_to_all(raw_scores.reshape(peer_count, arrived.shape[1], cent_coun...]
    dot_general x1 -> x3, matrix products: 0.71 us -> 5.86 us  [the longest x1 3.08 us: body(): jnp.dot(one_hot(wanted.reshape(-1), row_count), messages, preferred_eleme...]
    gather x2 -> x0, local copies, waits for them, and re-layouts: 3.94 us -> none  [the longest x1 2.79 us: body(): outgoing_msgs = jnp.take(messages, wanted.reshape(-1), axis=0)]
    all_to_all x1, waiting for transfers between devices: 12.5 us -> 9.06 us  [body(): lax.all_to_all(outgoing_msgs.reshape(peer_count, fetch_slots, width), 'in...]
    select_n x3 -> x0, other arithmetic: 3.23 us -> none  [the longest x2 2.47 us: body(): outgoing_msgs = jnp.take(messages, wanted.reshape(-1), axis=0)]
  transfers between devices with their start and end apart: 3 -> 1, of which waited for: 3 -> 1; matrix products, arithmetic and copies ran while one was open for 11% -> 8% of each run, Pallas kernels for 0% -> 0%
where the time goes in v2:
time: 93.7 us; the launch traced here: 93.3 us
  blocking collectives  59.9 us (64%)
  matrix products  12.8 us (14%)
  waiting for transfers between devices  9.06 us (10%)
  starting transfers between devices  5.29 us (6%)
  other arithmetic  5.13 us (5%)
  local copies, waits for them, and re-layouts  1.01 us (1%)
    all_gather x1, blocking collectives, body(): all_requests = lax.all_gather(requests[0], 'index', axis=0, tiled=False)  26.6 us
    all_to_all x1, blocking collectives, body(): lax.all_to_all(outgoing, 'index', split_axis=0, concat_axis=0, tiled=True)  20.6 us
    all_to_all x1, blocking collectives, body(): lax.all_to_all(raw_scores.reshape(peer_count, arrived.shape[1], cent_coun...  12.7 us
    all_to_all x1, waiting for transfers between devices, body(): lax.all_to_all(outgoing_msgs.reshape(peer_count, fetch_slots, width), 'in...  9.06 us
    all_to_all x1, starting transfers between devices, body(): lax.all_to_all(outgoing_msgs.reshape(peer_count, fetch_slots, width), 'in...  5.29 us
    reduce_sum x1, other arithmetic, body(): jnp.sum(jnp.where(slots[:, :, None] == slot_ids[None, None, :], weights_n...  4.35 us
    dot_general x1, matrix products, body(): jnp.dot(pooled, w_neigh, preferred_element_type=jnp.float32)  3.98 us
    dot_general x1, matrix products, body(): jnp.dot(one_hot(wanted.reshape(-1), row_count), messages, preferred_eleme...  3.08 us
  transfers between devices with their start and end apart: 1, of which 1 were waited for; matrix products, arithmetic and copies ran while one was open for 8% of the time, Pallas kernels for 0%

profile of v2, /device:TPU:1, one launch (start us, length us, event | category | flops | bytes accessed | tf_op | source)
XLA Modules:
  0.0 93.3 jit_solution(16191266868766386612)
XLA Ops:
  0.0 0.0 copy-start
  0.0 26.6 %all_gather.3 = s32[32,32,16]{1,2,0:T(8,128)S(1)} all-gather(s32[1,32,16]{1,2,0:T(8,128)} %param.18), channel_id=1, replica_groups=mesh['graph'=8,'index'=32] {'index'}, dimensions={0}, use_global_device_ids=true | all-gather | bytes 67584 | tf_op jit(solution)/shard_map/all_gather | solution.py:40
  26.6 0.7 dynamic-slice_reduce_fusion
  27.3 0.1 eq.83
  27.4 0.0 copy-done
  27.4 3.1 %convolution_convert_fusion.1 = bf16[512,1024]{1,0:T(8,128)(2,1)} fusion(bf16[256,1024]{1,0:T(8,128)(2,1)} %param.11, bf16[1024,1024]{1,0:T(8,128)(2,1)S(1)} %copy-done, f32[1024]{0:T(1024)} %param.13, s32[512]{0:T(512)S(1)} %eq.83), kind=kOutput, calls=%fused_computation.3 | convolution fusion | flops 806748160 | bytes 3676160 | tf_op jit(solution)/shard_map/dot_general | solution.py:51
  30.5 0.0 copy-start.3
  30.5 5.3 %all-to-all-start = ((bf16[32,16,1024]{2,1,0:T(8,128)(2,1)}), bf16[32,16,1024]{2,1,0:T(8,128)(2,1)}, u32[]{:S(2)}, u32[]{:S(2)}) async-start(bf16[32,16,1024]{2,1,0:T(8,128)(2,1)} %bitcast.5), calls=%async_computation | async-start | bytes 2097152 | tf_op jit(solution)/shard_map/all_to_all | solution.py:54
  35.8 0.0 copy-start.1
  35.8 0.0 copy-start.2
  35.8 0.0 copy-done.3
  35.8 0.6 reduce-window.6
  36.4 0.2 slice_reduce_fusion
  36.7 0.0 copy-start.5
  36.7 2.5 %fusion.16 = f32[256,1024]{1,0:T(8,128)S(1)} fusion(bf16[256,1024]{1,0:T(8,128)(2,1)} %param.11, bf16[1024,1024]{1,0:T(8,128)(2,1)} %param.14), kind=kOutput, calls=%fused_computation.37 | convolution fusion | flops 536870912 | bytes 3670016 | tf_op jit(solution)/shard_map/dot_general | solution.py:63
  39.2 0.1 fusion.13
  39.3 0.0 copy-done.1
  39.3 0.0 copy-done.2
  39.3 4.3 %select_reduce_fusion = bf16[256,512]{1,0:T(8,128)(2,1)S(1)} fusion(f32[256,50]{0,1:T(8,128)S(1)} %broadcast_divide_fusion, s32[256,50]{0,1:T(8,128)S(1)} %copy-done.2), kind=kLoop, calls=%fused_computation | loop fusion | flops 19529728 | bytes 364544 | tf_op jit(solution)/shard_map/reduce_sum | solution.py:46
  43.7 9.1 %all-to-all-done = bf16[32,16,1024]{2,1,0:T(8,128)(2,1)} async-done(((bf16[32,16,1024]{2,1,0:T(8,128)(2,1)}), bf16[32,16,1024]{2,1,0:T(8,128)(2,1)}, u32[]{:S(2)}, u32[]{:S(2)}) %all-to-all-start) | async-done | bytes 1048608 | tf_op jit(solution)/shard_map/all_to_all | solution.py:54
  52.7 0.0 copy-done.5
  52.7 4.0 %multiply_reduce_fusion = (f32[256]{0:T(256)S(1)}, f32[256,1024]{1,0:T(8,128)}) fusion(f32[1024]{0:T(1024)S(1)} %copy-done.5, f32[256,1024]{1,0:T(8,128)S(1)} %fusion.16, bf16[1024,1024]{1,0:T(8,128)(2,1)} %param.15, bf16[512,1024]{1,0:T(8,128)(2,1)} %bitcast.6, bf16[256,512]{1,0:T(8,128)(2,1)S(1)} %select_reduce_fusion), kind=kOutput, calls=%fused_computation.14 | convolution fusion | flops 806878976 | bytes 5510144 | tf_op jit(solution)/shard_map/dot_general | solution.py:64
  56.7 0.0 copy-start.4
  56.7 1.8 %convolution_convert_fusion = bf16[512,1024]{1,0:T(8,128)(2,1)S(1)} fusion(f32[256,1024]{1,0:T(8,128)} %get-tuple-element.6, f32[256]{0:T(256)S(1)} %add_rsqrt_fusion, s32[256]{0:T(256)S(1)} %bitcast.41), kind=kOutput, calls=%fused_computation.2 | convolution fusion | flops 269615104 | bytes 2099200 | tf_op jit(solution)/shard_map/dot_general | solution.py:72
  58.6 20.6 %all_to_all.15 = bf16[32,16,1024]{2,1,0:T(8,128)(2,1)S(1)} all-to-all(bf16[32,16,1024]{2,1,0:T(8,128)(2,1)S(1)} %bitcast.35), channel_id=1, replica_groups=mesh['graph'=8,'index'=32] {'index'}, dimensions={0} | all-to-all | bytes 2097152 | tf_op jit(solution)/shard_map/all_to_all | solution.py:76
  79.2 0.0 copy-done.4
  79.2 0.5 convolution_convert_fusion.3
  79.7 12.7 %all_to_all.16 = bf16[32,16,256]{2,1,0:T(8,128)(2,1)S(1)} all-to-all(bf16[32,16,256]{2,1,0:T(8,128)(2,1)S(1)} %bitcast.38), channel_id=1, replica_groups=mesh['graph'=8,'index'=32] {'index'}, dimensions={0} | all-to-all | bytes 524288 | tf_op jit(solution)/shard_map/all_to_all | solution.py:81
  92.4 0.9 %convolution_convert_fusion.4 = bf16[256,256]{1,0:T(8,128)(2,1)} fusion(bf16[512,256]{1,0:T(8,128)(2,1)S(1)} %bitcast.37, s32[256]{0:T(256)S(1)} %bitcast.42), kind=kOutput, calls=%fused_computation.12 | convolution fusion | flops 67305472 | bytes 394240 | tf_op jit(solution)/shard_map/dot_general | solution.py:88
  (7 shorter events, 0.1 us)
Async XLA Ops:
  0.0 27.4 %copy-start = (bf16[1024,1024]{1,0:T(8,128)(2,1)S(1)}, bf16[1024,1024]{1,0:T(8,128)(2,1)}, u32[]{:S(2)}) copy-start(bf16[1024,1024]{1,0:T(8,128)(2,1)} %param.12) | copy-start | bytes 6291460
  30.5 5.3 %copy-start.3 = (s32[256,1]{0,1:T(1,128)S(1)}, s32[256,1]{0,1:T(1,128)}, u32[]{:S(2)}) copy-start(s32[256,1]{0,1:T(1,128)} %param.21) | copy-start | bytes 3076
  30.5 22.3 %all-to-all-start = ((bf16[32,16,1024]{2,1,0:T(8,128)(2,1)}), bf16[32,16,1024]{2,1,0:T(8,128)(2,1)}, u32[]{:S(2)}, u32[]{:S(2)}) async-start(bf16[32,16,1024]{2,1,0:T(8,128)(2,1)} %bitcast.5), calls=%async_computation | async-start | bytes 2097152 | tf_op jit(solution)/shard_map/all_to_all | solution.py:54
  35.8 3.5 %copy-start.1 = (f32[256,50]{0,1:T(8,128)S(1)}, f32[256,50]{0,1:T(8,128)}, u32[]{:S(2)}) copy-start(f32[256,50]{0,1:T(8,128)} %param.20) | copy-start | bytes 153604
  35.8 3.5 %copy-start.2 = (s32[256,50]{0,1:T(8,128)S(1)}, s32[256,50]{0,1:T(8,128)}, u32[]{:S(2)}) copy-start(s32[256,50]{0,1:T(8,128)} %param.19) | copy-start | bytes 153604
  36.7 16.1 %copy-start.5 = (f32[1024]{0:T(1024)S(1)}, f32[1024]{0:T(1024)}, u32[]{:S(2)}) copy-start(f32[1024]{0:T(1024)} %param.16) | copy-start | bytes 12292
  56.7 22.5 %copy-start.4 = (bf16[256,1024]{1,0:T(8,128)(2,1)S(1)}, bf16[256,1024]{1,0:T(8,128)(2,1)}, u32[]{:S(2)}) copy-start(bf16[256,1024]{1,0:T(8,128)(2,1)} %param.17) | copy-start | bytes 1572868

commit v3 on v2

--- a/solution.py
+++ b/solution.py
@@ -36,8 +36,7 @@
     fetch_slots = requests.shape[2]
     slot_count = peer_count * fetch_slots
     cent_count = centroids.shape[0]
-    me = lax.axis_index("index")
-    all_requests = lax.all_gather(requests[0], "index", axis=0, tiled=False)
+    wanted = lax.all_to_all(requests, "index", split_axis=1, concat_axis=1, tiled=True)[0]
     messages = jax.nn.relu(
         jnp.dot(features, q_weight, preferred_element_type=jnp.float32) + q_bias
     ).astype(jnp.bfloat16)
@@ -47,7 +46,6 @@
         jnp.where(slots[:, :, None] == slot_ids[None, None, :], weights_norm[:, :, None], 0.0),
         axis=1,
     ).astype(jnp.bfloat16)
-    wanted = lax.dynamic_index_in_dim(all_requests, me, axis=1, keepdims=False)
     outgoing_msgs = jnp.dot(
         one_hot(wanted.reshape(-1), row_count), messages, preferred_element_type=jnp.float32
     ).astype(jnp.bfloat16)

time: 93.7 us -> 84.5 us (0.902)
  blocking collectives: 59.9 us -> 33.3 us
  starting transfers between devices: 5.29 us -> 13.6 us
  waiting for transfers between devices: 9.06 us -> 15.4 us
  other arithmetic: 5.13 us -> 6.47 us
  local copies, waits for them, and re-layouts: 1.01 us -> 2.34 us
    all_gather x1 -> x0, blocking collectives: 26.6 us -> none  [body(): all_requests = lax.all_gather(requests[0], 'index', axis=0, tiled=False)]
    all_to_all x0 -> x1, starting transfers between devices: none -> 8.58 us  [body(): lax.all_to_all(requests, 'index', split_axis=1, concat_axis=1, tiled=True)]
    all_to_all x1, waiting for transfers between devices: 9.06 us -> 12.6 us  [body(): lax.all_to_all(outgoing_msgs.reshape(peer_count, fetch_slots, width), 'in...]
    all_to_all x0 -> x1, waiting for transfers between devices: none -> 2.81 us  [body(): lax.all_to_all(requests, 'index', split_axis=1, concat_axis=1, tiled=True)]
    unnamed x12 -> x15, local copies, waits for them, and re-layouts: 0.03 us -> 1.56 us
  transfers between devices with their start and end apart: 1 -> 2, of which waited for: 1 -> 2; matrix products, arithmetic and copies ran while one was open for 8% -> 10% of each run, Pallas kernels for 0% -> 0%
where the time goes in v3:
time: 84.5 us; the launch traced here: 84 us
  blocking collectives  33.3 us (39%)
  waiting for transfers between devices  15.4 us (18%)
  starting transfers between devices  13.6 us (16%)
  matrix products  12.8 us (15%)
  other arithmetic  6.47 us (8%)
  local copies, waits for them, and re-layouts  2.34 us (3%)
    all_to_all x1, blocking collectives, body(): lax.all_to_all(outgoing, 'index', split_axis=0, concat_axis=0, tiled=True)  20.6 us
    all_to_all x1, blocking collectives, body(): lax.all_to_all(raw_scores.reshape(peer_count, arrived.shape[1], cent_coun...  12.7 us
    all_to_all x1, waiting for transfers between devices, body(): lax.all_to_all(outgoing_msgs.reshape(peer_count, fetch_slots, width), 'in...  12.6 us
    all_to_all x1, starting transfers between devices, body(): lax.all_to_all(requests, 'index', split_axis=1, concat_axis=1, tiled=True)  8.58 us
    all_to_all x1, starting transfers between devices, body(): lax.all_to_all(outgoing_msgs.reshape(peer_count, fetch_slots, width), 'in...  5.03 us
    reduce_sum x1, other arithmetic, body(): jnp.sum(jnp.where(slots[:, :, None] == slot_ids[None, None, :], weights_n...  4.35 us
    dot_general x1, matrix products, body(): jnp.dot(pooled, w_neigh, preferred_element_type=jnp.float32)  3.97 us
    dot_general x1, matrix products, body(): jnp.dot(one_hot(wanted.reshape(-1), row_count), messages, preferred_eleme...  3.06 us
  transfers between devices with their start and end apart: 2, of which 2 were waited for; matrix products, arithmetic and copies ran while one was open for 10% of the time, Pallas kernels for 0%

profile of v3, /device:TPU:1, one launch (start us, length us, event | category | flops | bytes accessed | tf_op | source)
XLA Modules:
  0.0 84.0 jit_solution(3445806696920112600)
XLA Ops:
  0.0 0.0 copy-start
  0.0 0.0 copy-start.3
  0.0 0.0 copy-start.5
  0.0 1.5 %copy.23 = s32[1,32,16]{2,0,1:T(1,128)} copy(s32[1,32,16]{1,2,0:T(8,128)} %param.18) | data formatting | bytes 4096 | tf_op args[7]
  1.5 8.6 %all-to-all-start = ((s32[1,32,16]{2,0,1:T(1,128)}), s32[1,32,16]{2,0,1:T(1,128)S(1)}, u32[]{:S(2)}, u32[]{:S(2)}) async-start(s32[1,32,16]{2,0,1:T(1,128)} %copy.23), calls=%async_computation | async-start | bytes 32768 | tf_op jit(solution)/shard_map/all_to_all | solution.py:39
  10.1 0.7 fusion.14
  10.8 0.6 reduce-window.6
  11.4 0.2 slice_reduce_fusion
  11.6 2.5 %fusion.16 = f32[256,1024]{1,0:T(8,128)S(1)} fusion(bf16[256,1024]{1,0:T(8,128)(2,1)} %param.11, bf16[1024,1024]{1,0:T(8,128)(2,1)} %param.14), kind=kOutput, calls=%fused_computation.36 | convolution fusion | flops 536870912 | bytes 3670016 | tf_op jit(solution)/shard_map/dot_general | solution.py:61
  14.1 0.0 copy-done.3
  14.1 0.1 fusion.13
  14.2 2.8 %all-to-all-done = s32[1,32,16]{2,0,1:T(1,128)S(1)} async-done(((s32[1,32,16]{2,0,1:T(1,128)}), s32[1,32,16]{2,0,1:T(1,128)S(1)}, u32[]{:S(2)}, u32[]{:S(2)}) %all-to-all-start) | async-done | bytes 2080 | tf_op jit(solution)/shard_map/all_to_all | solution.py:39
  17.0 0.5 broadcast.48
  17.5 0.7 reduce.5
  18.2 0.1 eq.83
  18.3 0.0 copy-done
  18.3 0.0 copy-done.5
  18.3 3.1 %convolution_convert_fusion.1 = bf16[512,1024]{1,0:T(8,128)(2,1)} fusion(bf16[256,1024]{1,0:T(8,128)(2,1)} %param.11, bf16[1024,1024]{1,0:T(8,128)(2,1)S(1)} %copy-done, f32[1024]{0:T(1024)S(1)} %copy-done.5, s32[512]{0:T(512)S(1)} %eq.83), kind=kOutput, calls=%fused_computation.3 | convolution fusion | flops 806748160 | bytes 3676160 | tf_op jit(solution)/shard_map/dot_general | solution.py:49
  21.4 0.0 copy-start.1
  21.4 5.0 %all-to-all-start.1 = ((bf16[32,16,1024]{2,1,0:T(8,128)(2,1)}), bf16[32,16,1024]{2,1,0:T(8,128)(2,1)}, u32[]{:S(2)}, u32[]{:S(2)}) async-start(bf16[32,16,1024]{2,1,0:T(8,128)(2,1)} %bitcast.37), calls=%async_computation.1 | async-start | bytes 2097152 | tf_op jit(solution)/shard_map/all_to_all | solution.py:52
  26.4 0.0 copy-done.1
  26.5 0.0 copy-done.2
  26.5 4.3 %select_reduce_fusion = bf16[256,512]{1,0:T(8,128)(2,1)S(1)} fusion(f32[256,50]{0,1:T(8,128)S(1)} %broadcast_divide_fusion, s32[256,50]{0,1:T(8,128)S(1)} %copy-done.2), kind=kLoop, calls=%fused_computation | loop fusion | flops 19529728 | bytes 364544 | tf_op jit(solution)/shard_map/reduce_sum | solution.py:45
  30.9 12.6 %all-to-all-done.1 = bf16[32,16,1024]{2,1,0:T(8,128)(2,1)} async-done(((bf16[32,16,1024]{2,1,0:T(8,128)(2,1)}), bf16[32,16,1024]{2,1,0:T(8,128)(2,1)}, u32[]{:S(2)}, u32[]{:S(2)}) %all-to-all-start.1) | async-done | bytes 1048608 | tf_op jit(solution)/shard_map/all_to_all | solution.py:52
  43.5 0.0 copy-done.6
  43.5 4.0 %multiply_reduce_fusion = (f32[256]{0:T(256)S(1)}, f32[256,1024]{1,0:T(8,128)}) fusion(f32[1024]{0:T(1024)S(1)} %copy-done.6, f32[256,1024]{1,0:T(8,128)S(1)} %fusion.16, bf16[1024,1024]{1,0:T(8,128)(2,1)} %param.15, bf16[512,1024]{1,0:T(8,128)(2,1)} %bitcast.6, bf16[256,512]{1,0:T(8,128)(2,1)S(1)} %select_reduce_fusion), kind=kOutput, calls=%fused_computation.14 | convolution fusion | flops 806878976 | bytes 5510144 | tf_op jit(solution)/shard_map/dot_general | solution.py:62
  47.5 1.8 %convolution_convert_fusion = bf16[512,1024]{1,0:T(8,128)(2,1)S(1)} fusion(f32[256,1024]{1,0:T(8,128)} %get-tuple-element.6, f32[256]{0:T(256)S(1)} %add_rsqrt_fusion, s32[256]{0:T(256)S(1)} %bitcast.43), kind=kOutput, calls=%fused_computation.2 | convolution fusion | flops 269615104 | bytes 2099200 | tf_op jit(solution)/shard_map/dot_general | solution.py:70
  49.3 20.6 %all_to_all.20 = bf16[32,16,1024]{2,1,0:T(8,128)(2,1)S(1)} all-to-all(bf16[32,16,1024]{2,1,0:T(8,128)(2,1)S(1)} %bitcast.36), channel_id=1, replica_groups=mesh['graph'=8,'index'=32] {'index'}, dimensions={0} | all-to-all | bytes 2097152 | tf_op jit(solution)/shard_map/all_to_all | solution.py:74
  69.9 0.0 copy-done.4
  69.9 0.5 convolution_convert_fusion.3
  70.4 12.7 %all_to_all.21 = bf16[32,16,256]{2,1,0:T(8,128)(2,1)S(1)} all-to-all(bf16[32,16,256]{2,1,0:T(8,128)(2,1)S(1)} %bitcast.40), channel_id=1, replica_groups=mesh['graph'=8,'index'=32] {'index'}, dimensions={0} | all-to-all | bytes 524288 | tf_op jit(solution)/shard_map/all_to_all | solution.py:79
  83.1 0.9 %convolution_convert_fusion.4 = bf16[256,256]{1,0:T(8,128)(2,1)} fusion(bf16[512,256]{1,0:T(8,128)(2,1)S(1)} %bitcast.39, s32[256]{0:T(256)S(1)} %bitcast.44), kind=kOutput, calls=%fused_computation.12 | convolution fusion | flops 67305472 | bytes 394240 | tf_op jit(solution)/shard_map/dot_general | solution.py:86
  (9 shorter events, 0.1 us)
Async XLA Ops:
  0.0 18.3 %copy-start = (bf16[1024,1024]{1,0:T(8,128)(2,1)S(1)}, bf16[1024,1024]{1,0:T(8,128)(2,1)}, u32[]{:S(2)}) copy-start(bf16[1024,1024]{1,0:T(8,128)(2,1)} %param.12) | copy-start | bytes 6291460
  0.0 14.1 %copy-start.3 = (s32[256,1]{0,1:T(1,128)S(1)}, s32[256,1]{0,1:T(1,128)}, u32[]{:S(2)}) copy-start(s32[256,1]{0,1:T(1,128)} %param.21) | copy-start | bytes 3076
  0.0 18.3 %copy-start.5 = (f32[1024]{0:T(1024)S(1)}, f32[1024]{0:T(1024)}, u32[]{:S(2)}) copy-start(f32[1024]{0:T(1024)} %param.13) | copy-start | bytes 12292
  1.5 15.5 %all-to-all-start = ((s32[1,32,16]{2,0,1:T(1,128)}), s32[1,32,16]{2,0,1:T(1,128)S(1)}, u32[]{:S(2)}, u32[]{:S(2)}) async-start(s32[1,32,16]{2,0,1:T(1,128)} %copy.23), calls=%async_computation | async-start | bytes 32768 | tf_op jit(solution)/shard_map/all_to_all | solution.py:39
  21.4 5.1 %copy-start.1 = (f32[256,50]{0,1:T(8,128)S(1)}, f32[256,50]{0,1:T(8,128)}, u32[]{:S(2)}) copy-start(f32[256,50]{0,1:T(8,128)} %param.20) | copy-start | bytes 153604
  21.4 5.1 %copy-start.2 = (s32[256,50]{0,1:T(8,128)S(1)}, s32[256,50]{0,1:T(8,128)}, u32[]{:S(2)}) copy-start(s32[256,50]{0,1:T(8,128)} %param.19) | copy-start | bytes 153604
  21.4 22.1 %copy-start.6 = (f32[1024]{0:T(1024)S(1)}, f32[1024]{0:T(1024)}, u32[]{:S(2)}) copy-start(f32[1024]{0:T(1024)} %param.16) | copy-start | bytes 12292
  21.4 22.1 %all-to-all-start.1 = ((bf16[32,16,1024]{2,1,0:T(8,128)(2,1)}), bf16[32,16,1024]{2,1,0:T(8,128)(2,1)}, u32[]{:S(2)}, u32[]{:S(2)}) async-start(bf16[32,16,1024]{2,1,0:T(8,128)(2,1)} %bitcast.37), calls=%async_computation.1 | async-start | bytes 2097152 | tf_op jit(solution)/shard_map/all_to_all | solution.py:52
  47.5 22.5 %copy-start.4 = (bf16[256,1024]{1,0:T(8,128)(2,1)S(1)}, bf16[256,1024]{1,0:T(8,128)(2,1)}, u32[]{:S(2)}) copy-start(bf16[256,1024]{1,0:T(8,128)(2,1)} %param.17) | copy-start | bytes 1572868

commit v4 on v3

--- a/solution.py
+++ b/solution.py
@@ -47,7 +47,9 @@
         axis=1,
     ).astype(jnp.bfloat16)
     outgoing_msgs = jnp.dot(
-        one_hot(wanted.reshape(-1), row_count), messages, preferred_element_type=jnp.float32
+        one_hot(wanted.reshape(-1), row_count),
+        lax.optimization_barrier(messages),
+        preferred_element_type=jnp.float32,
     ).astype(jnp.bfloat16)
     fetched = lax.all_to_all(
         outgoing_msgs.reshape(peer_count, fetch_slots, width),

time: 84.5 us -> 84.5 us (level)
  waiting for transfers between devices: 15.4 us -> 13.7 us
  starting transfers between devices: 13.6 us -> 14.9 us
    all_to_all x1, waiting for transfers between devices: 2.81 us -> 1.13 us  [body(): lax.all_to_all(requests, 'index', split_axis=1, concat_axis=1, tiled=True)]
    all_to_all x1, starting transfers between devices: 5.03 us -> 6.31 us  [body(): lax.all_to_all(outgoing_msgs.reshape(peer_count, fetch_slots, width), 'in...]
    dot_general x1 -> x2, matrix products: 3.06 us -> 4.08 us  [the longest x1 2.58 us: body(): jnp.dot(one_hot(wanted.reshape(-1), row_count), lax.optimization_barrier(...]
  transfers between devices with their start and end apart: 2 -> 2, of which waited for: 2 -> 2; matrix products, arithmetic and copies ran while one was open for 10% -> 12% of each run, Pallas kernels for 0% -> 0%
where the time goes in v4:
time: 84.5 us; the launch traced here: 84.1 us
  blocking collectives  33.3 us (39%)
  starting transfers between devices  14.9 us (18%)
  waiting for transfers between devices  13.7 us (16%)
  matrix products  13.2 us (16%)
  other arithmetic  6.47 us (8%)
  local copies, waits for them, and re-layouts  2.35 us (3%)
    all_to_all x1, blocking collectives, body(): lax.all_to_all(outgoing, 'index', split_axis=0, concat_axis=0, tiled=True)  20.6 us
    all_to_all x1, blocking collectives, body(): lax.all_to_all(raw_scores.reshape(peer_count, arrived.shape[1], cent_coun...  12.7 us
    all_to_all x1, waiting for transfers between devices, body(): lax.all_to_all(outgoing_msgs.reshape(peer_count, fetch_slots, width), 'in...  12.5 us
    all_to_all x1, starting transfers between devices, body(): lax.all_to_all(requests, 'index', split_axis=1, concat_axis=1, tiled=True)  8.58 us
    all_to_all x1, starting transfers between devices, body(): lax.all_to_all(outgoing_msgs.reshape(peer_count, fetch_slots, width), 'in...  6.31 us
    reduce_sum x1, other arithmetic, body(): jnp.sum(jnp.where(slots[:, :, None] == slot_ids[None, None, :], weights_n...  4.35 us
    dot_general x1, matrix products, body(): jnp.dot(pooled, w_neigh, preferred_element_type=jnp.float32)  3.28 us
    dot_general x1, matrix products, body(): jnp.dot(features, w_self, preferred_element_type=jnp.float32)  2.61 us
  transfers between devices with their start and end apart: 2, of which 2 were waited for; matrix products, arithmetic and copies ran while one was open for 12% of the time, Pallas kernels for 0%

profile of v4, /device:TPU:1, one launch (start us, length us, event | category | flops | bytes accessed | tf_op | source)
XLA Modules:
  0.0 84.1 jit_solution(3257541548949189680)
XLA Ops:
  0.0 0.0 copy-start
  0.0 1.5 %copy.23 = s32[1,32,16]{2,0,1:T(1,128)} copy(s32[1,32,16]{1,2,0:T(8,128)} %param.18) | data formatting | bytes 4096 | tf_op args[7]
  1.5 8.6 %all-to-all-start = ((s32[1,32,16]{2,0,1:T(1,128)}), s32[1,32,16]{2,0,1:T(1,128)S(1)}, u32[]{:S(2)}, u32[]{:S(2)}) async-start(s32[1,32,16]{2,0,1:T(1,128)} %copy.23), calls=%async_computation | async-start | bytes 32768 | tf_op jit(solution)/shard_map/all_to_all | solution.py:39
  10.1 0.7 fusion.12
  10.8 0.6 reduce-window.6
  11.4 0.2 slice_reduce_fusion
  11.6 2.6 %fusion.13 = f32[256,1024]{1,0:T(8,128)S(1)} fusion(bf16[256,1024]{1,0:T(8,128)(2,1)} %param.11, bf16[1024,1024]{1,0:T(8,128)(2,1)} %param.14), kind=kOutput, calls=%fused_computation.33 | convolution fusion | flops 536870912 | bytes 3670016 | tf_op jit(solution)/shard_map/dot_general | solution.py:63
  14.2 0.0 copy-done.7
  14.3 0.0 copy-done.1
  14.3 0.0 copy-done.5
  14.3 0.0 copy-start.4
  14.3 1.5 %fusion.3 = bf16[256,1024]{1,0:T(8,128)(2,1)} fusion(bf16[256,1024]{1,0:T(8,128)(2,1)S(1)} %copy-done.1, bf16[1024,1024]{1,0:T(8,128)(2,1)S(1)} %copy-done.5, f32[1024]{0:T(1024)S(1)} %copy-done.7), kind=kOutput, calls=%fused_computation.9 | convolution fusion | flops 537657344 | bytes 3149824 | tf_op jit(solution)/shard_map/dot_general | solution.py:41
  15.8 0.0 copy-done.4
  15.8 0.1 fusion.11
  15.9 1.1 %all-to-all-done = s32[1,32,16]{2,0,1:T(1,128)S(1)} async-done(((s32[1,32,16]{2,0,1:T(1,128)}), s32[1,32,16]{2,0,1:T(1,128)S(1)}, u32[]{:S(2)}, u32[]{:S(2)}) %all-to-all-start) | async-done | bytes 2080 | tf_op jit(solution)/shard_map/all_to_all | solution.py:39
  17.0 0.5 broadcast.48
  17.5 0.7 reduce.5
  18.2 0.1 eq.83
  18.3 2.6 %convolution_convert_fusion.1 = bf16[512,1024]{1,0:T(8,128)(2,1)} fusion(bf16[256,1024]{1,0:T(8,128)(2,1)} %fusion.3, s32[512]{0:T(512)S(1)} %eq.83), kind=kOutput, calls=%fused_computation.3 | convolution fusion | flops 269090816 | bytes 1574912 | tf_op jit(solution)/shard_map/dot_general | solution.py:49
  20.9 6.3 %all-to-all-start.1 = ((bf16[32,16,1024]{2,1,0:T(8,128)(2,1)}), bf16[32,16,1024]{2,1,0:T(8,128)(2,1)}, u32[]{:S(2)}, u32[]{:S(2)}) async-start(bf16[32,16,1024]{2,1,0:T(8,128)(2,1)} %bitcast.5), calls=%async_computation.1 | async-start | bytes 2097152 | tf_op jit(solution)/shard_map/all_to_all | solution.py:54
  27.2 0.0 copy-done.2
  27.3 0.0 copy-done.3
  27.3 4.3 %select_reduce_fusion = bf16[256,512]{1,0:T(8,128)(2,1)S(1)} fusion(f32[256,50]{0,1:T(8,128)S(1)} %broadcast_divide_fusion, s32[256,50]{0,1:T(8,128)S(1)} %copy-done.3), kind=kLoop, calls=%fused_computation | loop fusion | flops 19529728 | bytes 364544 | tf_op jit(solution)/shard_map/reduce_sum | solution.py:45
  31.6 12.5 %all-to-all-done.1 = bf16[32,16,1024]{2,1,0:T(8,128)(2,1)} async-done(((bf16[32,16,1024]{2,1,0:T(8,128)(2,1)}), bf16[32,16,1024]{2,1,0:T(8,128)(2,1)}, u32[]{:S(2)}, u32[]{:S(2)}) %all-to-all-start.1) | async-done | bytes 1048608 | tf_op jit(solution)/shard_map/all_to_all | solution.py:54
  44.2 0.0 copy-done
  44.2 0.0 copy-done.8
  44.2 3.3 %multiply_reduce_fusion = (f32[256]{0:T(256)S(1)}, f32[256,1024]{1,0:T(8,128)}) fusion(f32[1024]{0:T(1024)S(1)} %copy-done.8, f32[256,1024]{1,0:T(8,128)S(1)} %fusion.13, bf16[1024,1024]{1,0:T(8,128)(2,1)S(1)} %copy-done, bf16[512,1024]{1,0:T(8,128)(2,1)} %bitcast.6, bf16[256,512]{1,0:T(8,128)(2,1)S(1)} %select_reduce_fusion), kind=kOutput, calls=%fused_computation.14 | convolution fusion | flops 806878976 | bytes 5510144 | tf_op jit(solution)/shard_map/dot_general | solution.py:64
  47.5 1.8 %convolution_convert_fusion = bf16[512,1024]{1,0:T(8,128)(2,1)S(1)} fusion(f32[256,1024]{1,0:T(8,128)} %get-tuple-element.6, f32[256]{0:T(256)S(1)} %add_rsqrt_fusion, s32[256]{0:T(256)S(1)} %bitcast.43), kind=kOutput, calls=%fused_computation.2 | convolution fusion | flops 269615104 | bytes 2099200 | tf_op jit(solution)/shard_map/dot_general | solution.py:72
  49.3 20.6 %all_to_all.20 = bf16[32,16,1024]{2,1,0:T(8,128)(2,1)S(1)} all-to-all(bf16[32,16,1024]{2,1,0:T(8,128)(2,1)S(1)} %bitcast.37), channel_id=1, replica_groups=mesh['graph'=8,'index'=32] {'index'}, dimensions={0} | all-to-all | bytes 2097152 | tf_op jit(solution)/shard_map/all_to_all | solution.py:76
  70.0 0.5 convolution_convert_fusion.3
  70.4 12.7 %all_to_all.21 = bf16[32,16,256]{2,1,0:T(8,128)(2,1)S(1)} all-to-all(bf16[32,16,256]{2,1,0:T(8,128)(2,1)S(1)} %bitcast.40), channel_id=1, replica_groups=mesh['graph'=8,'index'=32] {'index'}, dimensions={0} | all-to-all | bytes 524288 | tf_op jit(solution)/shard_map/all_to_all | solution.py:81
  83.1 0.9 %convolution_convert_fusion.4 = bf16[256,256]{1,0:T(8,128)(2,1)} fusion(bf16[512,256]{1,0:T(8,128)(2,1)S(1)} %bitcast.39, s32[256]{0:T(256)S(1)} %bitcast.44), kind=kOutput, calls=%fused_computation.12 | convolution fusion | flops 67305472 | bytes 394240 | tf_op jit(solution)/shard_map/dot_general | solution.py:88
  (14 shorter events, 0.1 us)
Async XLA Ops:
  0.0 44.2 %copy-start = (bf16[1024,1024]{1,0:T(8,128)(2,1)S(1)}, bf16[1024,1024]{1,0:T(8,128)(2,1)}, u32[]{:S(2)}) copy-start(bf16[1024,1024]{1,0:T(8,128)(2,1)} %param.15) | copy-start | bytes 6291460
  0.0 14.2 %copy-start.7 = (f32[1024]{0:T(1024)S(1)}, f32[1024]{0:T(1024)}, u32[]{:S(2)}) copy-start(f32[1024]{0:T(1024)} %param.13) | copy-start | bytes 12292
  1.5 15.5 %all-to-all-start = ((s32[1,32,16]{2,0,1:T(1,128)}), s32[1,32,16]{2,0,1:T(1,128)S(1)}, u32[]{:S(2)}, u32[]{:S(2)}) async-start(s32[1,32,16]{2,0,1:T(1,128)} %copy.23), calls=%async_computation | async-start | bytes 32768 | tf_op jit(solution)/shard_map/all_to_all | solution.py:39
  11.6 2.6 %copy-start.1 = (bf16[256,1024]{1,0:T(8,128)(2,1)S(1)}, bf16[256,1024]{1,0:T(8,128)(2,1)}, u32[]{:S(2)}) copy-start(bf16[256,1024]{1,0:T(8,128)(2,1)} %param.11) | copy-start | bytes 1572868
  11.6 2.7 %copy-start.5 = (bf16[1024,1024]{1,0:T(8,128)(2,1)S(1)}, bf16[1024,1024]{1,0:T(8,128)(2,1)}, u32[]{:S(2)}) copy-start(bf16[1024,1024]{1,0:T(8,128)(2,1)} %param.12) | copy-start | bytes 6291460
  14.3 1.5 %copy-start.4 = (s32[256,1]{0,1:T(1,128)S(1)}, s32[256,1]{0,1:T(1,128)}, u32[]{:S(2)}) copy-start(s32[256,1]{0,1:T(1,128)} %param.21) | copy-start | bytes 3076
  15.8 11.4 %copy-start.2 = (f32[256,50]{0,1:T(8,128)S(1)}, f32[256,50]{0,1:T(8,128)}, u32[]{:S(2)}) copy-start(f32[256,50]{0,1:T(8,128)} %param.20) | copy-start | bytes 153604
  15.8 11.5 %copy-start.3 = (s32[256,50]{0,1:T(8,128)S(1)}, s32[256,50]{0,1:T(8,128)}, u32[]{:S(2)}) copy-start(s32[256,50]{0,1:T(8,128)} %param.19) | copy-start | bytes 153604
  18.3 25.9 %copy-start.8 = (f32[1024]{0:T(1024)S(1)}, f32[1024]{0:T(1024)}, u32[]{:S(2)}) copy-start(f32[1024]{0:T(1024)} %param.16) | copy-start | bytes 12292
  20.9 23.3 %all-to-all-start.1 = ((bf16[32,16,1024]{2,1,0:T(8,128)(2,1)}), bf16[32,16,1024]{2,1,0:T(8,128)(2,1)}, u32[]{:S(2)}, u32[]{:S(2)}) async-start(bf16[32,16,1024]{2,1,0:T(8,128)(2,1)} %bitcast.5), calls=%async_computation.1 | async-start | bytes 2097152 | tf_op jit(solution)/shard_map/all_to_all | solution.py:54
  47.5 22.5 %copy-start.6 = (bf16[256,1024]{1,0:T(8,128)(2,1)S(1)}, bf16[256,1024]{1,0:T(8,128)(2,1)}, u32[]{:S(2)}) copy-start(bf16[256,1024]{1,0:T(8,128)(2,1)} %param.17) | copy-start | bytes 1572868

commit v5 on v4

--- a/solution.py
+++ b/solution.py
@@ -36,7 +36,14 @@
     fetch_slots = requests.shape[2]
     slot_count = peer_count * fetch_slots
     cent_count = centroids.shape[0]
-    wanted = lax.all_to_all(requests, "index", split_axis=1, concat_axis=1, tiled=True)[0]
+    me = lax.axis_index("index")
+    own_rows = jnp.where(
+        jnp.arange(peer_count, dtype=jnp.int32)[:, None, None] == me,
+        requests.astype(jnp.float32),
+        0.0,
+    )
+    all_requests = lax.psum(own_rows, "index")
+    wanted = lax.dynamic_index_in_dim(all_requests, me, axis=1, keepdims=False).astype(jnp.int32)
     messages = jax.nn.relu(
         jnp.dot(features, q_weight, preferred_element_type=jnp.float32) + q_bias
     ).astype(jnp.bfloat16)

time: 84.5 us -> 202 us (2.39)
  waiting for transfers between devices: 13.7 us -> 126 us
  between operations: 0.15 us -> 13.5 us
  starting transfers between devices: 14.9 us -> 6.08 us
    psum x0 -> x1, waiting for transfers between devices: none -> 113 us  [body(): all_requests = lax.psum(own_rows, 'index')]
    all_to_all x1 -> x0, starting transfers between devices: 8.58 us -> none  [body(): lax.all_to_all(requests, 'index', split_axis=1, concat_axis=1, tiled=True)]
  transfers between devices with their start and end apart: 2 -> 2, of which waited for: 2 -> 2; matrix products, arithmetic and copies ran while one was open for 12% -> 6% of each run, Pallas kernels for 0% -> 0%
where the time goes in v5:
time: 202 us
  waiting for transfers between devices  126 us (62%)
  blocking collectives  33.3 us (16%)
  matrix products  14.3 us (7%)
  between operations  13.5 us (7%)
  other arithmetic  8.31 us (4%)
  starting transfers between devices  6.08 us (3%)
    psum x1, waiting for transfers between devices, body(): all_requests = lax.psum(own_rows, 'index')  113 us
    all_to_all x1, blocking collectives, body(): lax.all_to_all(outgoing, 'index', split_axis=0, concat_axis=0, tiled=True)  20.6 us
    all_to_all x1, blocking collectives, body(): lax.all_to_all(raw_scores.reshape(peer_count, arrived.shape[1], cent_coun...  12.7 us
    all_to_all x1, waiting for transfers between devices, body(): lax.all_to_all(outgoing_msgs.reshape(peer_count, fetch_slots, width), 'in...  12.5 us
    all_to_all x1, starting transfers between devices, body(): lax.all_to_all(outgoing_msgs.reshape(peer_count, fetch_slots, width), 'in...  6.08 us
    reduce_sum x1, other arithmetic, body(): jnp.sum(jnp.where(slots[:, :, None] == slot_ids[None, None, :], weights_n...  4.35 us
  transfers between devices with their start and end apart: 2, of which 2 were waited for; matrix products, arithmetic and copies ran while one was open for 6% of the time, Pallas kernels for 0%

profile of v5, /device:TPU:1, one launch (start us, length us, event | category | flops | bytes accessed | tf_op | source)
XLA Modules:
  0.0 201.9 jit_solution(17790053467064373194)
XLA Ops:
  6.5 0.0 copy-start
  6.5 0.0 all-reduce.2.cloned.1.call-start
  6.5 0.8 convert_bitcast_fusion
  7.4 0.1 copy.20
  7.5 0.9 broadcast_select_fusion
  8.4 0.0 all-reduce.2.cloned.1.call-update
  8.4 0.7 fusion.12
  9.1 0.6 reduce-window.6
  9.7 0.2 slice_reduce_fusion
  9.9 2.6 %fusion.13 = f32[256,1024]{1,0:T(8,128)S(1)} fusion(bf16[256,1024]{1,0:T(8,128)(2,1)} %param.11, bf16[1024,1024]{1,0:T(8,128)(2,1)} %param.14), kind=kOutput, calls=%fused_computation.37 | convolution fusion | flops 536870912 | bytes 3670016 | tf_op jit(solution)/shard_map/dot_general | solution.py:70
  12.6 0.0 copy-done.6
  12.6 0.0 copy-done.4
  12.6 0.0 copy-start.3
  12.6 2.6 %fusion.3 = bf16[256,1024]{1,0:T(8,128)(2,1)} fusion(bf16[256,1024]{1,0:T(8,128)(2,1)} %param.11, bf16[1024,1024]{1,0:T(8,128)(2,1)S(1)} %copy-done.4, f32[1024]{0:T(1024)S(1)} %copy-done.6), kind=kOutput, calls=%fused_computation.9 | convolution fusion | flops 537657344 | bytes 3149824 | tf_op jit(solution)/shard_map/dot_general | solution.py:48
  15.1 0.0 copy-done.3
  15.1 0.1 fusion.11
  15.2 113.5 %all-reduce.2.cloned.1.call-done = f32[32,32,16]{2,0,1:T(8,128)} async-done(((f32[32,32,16]{2,0,1:T(8,128)}), f32[32,32,16]{2,0,1:T(8,128)}) %all-reduce.2.cloned.1.call-update) | async-done | bytes 65552 | tf_op jit(solution)/shard_map/psum | solution.py:45
  128.7 0.7 dynamic-slice_convert_fusion
  129.4 0.1 convert_element_type.48
  129.5 2.6 %convolution_convert_fusion.1 = bf16[512,1024]{1,0:T(8,128)(2,1)} fusion(bf16[256,1024]{1,0:T(8,128)(2,1)} %fusion.3, s32[512]{0:T(512)S(1)} %convert_element_type.48), kind=kOutput, calls=%fused_computation.3 | convolution fusion | flops 269090816 | bytes 1574912 | tf_op jit(solution)/shard_map/dot_general | solution.py:56
  132.1 6.1 %all-to-all-start = ((bf16[32,16,1024]{2,1,0:T(8,128)(2,1)}), bf16[32,16,1024]{2,1,0:T(8,128)(2,1)}, u32[]{:S(2)}, u32[]{:S(2)}) async-start(bf16[32,16,1024]{2,1,0:T(8,128)(2,1)} %bitcast.6), calls=%async_computation | async-start | bytes 2097152 | tf_op jit(solution)/shard_map/all_to_all | solution.py:61
  138.2 0.0 copy-done.1
  138.3 0.0 copy-done.2
  138.3 4.3 %select_reduce_fusion = bf16[256,512]{1,0:T(8,128)(2,1)S(1)} fusion(f32[256,50]{0,1:T(8,128)S(1)} %broadcast_divide_fusion, s32[256,50]{0,1:T(8,128)S(1)} %copy-done.2), kind=kLoop, calls=%fused_computation | loop fusion | flops 19529728 | bytes 364544 | tf_op jit(solution)/shard_map/reduce_sum | solution.py:52
  142.6 12.5 %all-to-all-done = bf16[32,16,1024]{2,1,0:T(8,128)(2,1)} async-done(((bf16[32,16,1024]{2,1,0:T(8,128)(2,1)}), bf16[32,16,1024]{2,1,0:T(8,128)(2,1)}, u32[]{:S(2)}, u32[]{:S(2)}) %all-to-all-start) | async-done | bytes 1048608 | tf_op jit(solution)/shard_map/all_to_all | solution.py:61
  155.1 0.0 copy-done
  155.2 3.3 %multiply_reduce_fusion = (f32[256]{0:T(256)S(1)}, f32[256,1024]{1,0:T(8,128)}) fusion(f32[1024]{0:T(1024)S(1)} %copy-done.7, f32[256,1024]{1,0:T(8,128)S(1)} %fusion.13, bf16[1024,1024]{1,0:T(8,128)(2,1)S(1)} %copy-done, bf16[512,1024]{1,0:T(8,128)(2,1)} %bitcast.7, bf16[256,512]{1,0:T(8,128)(2,1)S(1)} %select_reduce_fusion), kind=kOutput, calls=%fused_computation.14 | convolution fusion | flops 806878976 | bytes 5510144 | tf_op jit(solution)/shard_map/dot_general | solution.py:71
  158.4 1.8 convolution_convert_fusion
  160.3 20.6 %all_to_all.15 = bf16[32,16,1024]{2,1,0:T(8,128)(2,1)S(1)} all-to-all(bf16[32,16,1024]{2,1,0:T(8,128)(2,1)S(1)} %bitcast.40), channel_id=1, replica_groups=mesh['graph'=8,'index'=32] {'index'}, dimensions={0} | all-to-all | bytes 2097152 | tf_op jit(solution)/shard_map/all_to_all | solution.py:83
  180.9 0.5 convolution_convert_fusion.3
  181.4 12.7 %all_to_all.16 = bf16[32,16,256]{2,1,0:T(8,128)(2,1)S(1)} all-to-all(bf16[32,16,256]{2,1,0:T(8,128)(2,1)S(1)} %bitcast.43), channel_id=1, replica_groups=mesh['graph'=8,'index'=32] {'index'}, dimensions={0} | all-to-all | bytes 524288 | tf_op jit(solution)/shard_map/all_to_all | solution.py:88
  194.1 0.9 convolution_convert_fusion.4
  (15 shorter events, 0.1 us)
Async XLA Ops:
  6.5 148.6 %copy-start = (bf16[1024,1024]{1,0:T(8,128)(2,1)S(1)}, bf16[1024,1024]{1,0:T(8,128)(2,1)}, u32[]{:S(2)}) copy-start(bf16[1024,1024]{1,0:T(8,128)(2,1)} %param.15) | copy-start | bytes 6291460
  6.5 122.2 %all-reduce.2.cloned.1.call-start = ((), (), s32[]{:S(2)}) async-start(), calls=%async_computation.3 | async-start | bytes 1048576 | tf_op jit(solution)/shard_map/psum | solution.py:45
  8.4 4.1 %copy-start.6 = (f32[1024]{0:T(1024)S(1)}, f32[1024]{0:T(1024)}, u32[]{:S(2)}) copy-start(f32[1024]{0:T(1024)} %param.13) | copy-start | bytes 12292
  9.9 2.6 %copy-start.4 = (bf16[1024,1024]{1,0:T(8,128)(2,1)S(1)}, bf16[1024,1024]{1,0:T(8,128)(2,1)}, u32[]{:S(2)}) copy-start(bf16[1024,1024]{1,0:T(8,128)(2,1)} %param.12) | copy-start | bytes 6291460
  12.6 2.6 %copy-start.3 = (s32[256,1]{0,1:T(1,128)S(1)}, s32[256,1]{0,1:T(1,128)}, u32[]{:S(2)}) copy-start(s32[256,1]{0,1:T(1,128)} %param.21) | copy-start | bytes 3076
  15.1 123.1 %copy-start.1 = (f32[256,50]{0,1:T(8,128)S(1)}, f32[256,50]{0,1:T(8,128)}, u32[]{:S(2)}) copy-start(f32[256,50]{0,1:T(8,128)} %param.20) | copy-start | bytes 153604
  15.1 123.1 %copy-start.2 = (s32[256,50]{0,1:T(8,128)S(1)}, s32[256,50]{0,1:T(8,128)}, u32[]{:S(2)}) copy-start(s32[256,50]{0,1:T(8,128)} %param.19) | copy-start | bytes 153604
  129.5 25.6 %copy-start.7 = (f32[1024]{0:T(1024)S(1)}, f32[1024]{0:T(1024)}, u32[]{:S(2)}) copy-start(f32[1024]{0:T(1024)} %param.16) | copy-start | bytes 12292
  132.1 23.0 %all-to-all-start = ((bf16[32,16,1024]{2,1,0:T(8,128)(2,1)}), bf16[32,16,1024]{2,1,0:T(8,128)(2,1)}, u32[]{:S(2)}, u32[]{:S(2)}) async-start(bf16[32,16,1024]{2,1,0:T(8,128)(2,1)} %bitcast.6), calls=%async_computation | async-start | bytes 2097152 | tf_op jit(solution)/shard_map/all_to_all | solution.py:61
  158.4 22.5 %copy-start.5 = (bf16[256,1024]{1,0:T(8,128)(2,1)S(1)}, bf16[256,1024]{1,0:T(8,128)(2,1)}, u32[]{:S(2)}) copy-start(bf16[256,1024]{1,0:T(8,128)(2,1)} %param.17) | copy-start | bytes 1572868
Sparse Core Ops, SparseCore 0:
  10.5 118.1 all-reduce.1

commit v6 on v3

--- a/solution.py
+++ b/solution.py
@@ -36,7 +36,7 @@
     fetch_slots = requests.shape[2]
     slot_count = peer_count * fetch_slots
     cent_count = centroids.shape[0]
-    wanted = lax.all_to_all(requests, "index", split_axis=1, concat_axis=1, tiled=True)[0]
+    wanted = lax.all_to_all(requests.astype(jnp.float32), "index", split_axis=1, concat_axis=1, tiled=True)[0].astype(jnp.int32)
     messages = jax.nn.relu(
         jnp.dot(features, q_weight, preferred_element_type=jnp.float32) + q_bias
     ).astype(jnp.bfloat16)
@@ -56,7 +56,8 @@
         concat_axis=0,
         tiled=True,
     ).reshape(slot_count, width)
-    pooled = jnp.dot(mixing, fetched, preferred_element_type=jnp.float32).astype(jnp.bfloat16)
+    pooled = lax.optimization_barrier(
+        jnp.dot(mixing, fetched, preferred_element_type=jnp.float32).astype(jnp.bfloat16))
     hidden = jax.nn.relu(
         jnp.dot(features, w_self, preferred_element_type=jnp.float32)
         + jnp.dot(pooled, w_neigh, preferred_element_type=jnp.float32)

time: 84.5 us -> 80.7 us (0.955)
  matrix products: 12.8 us -> 10.6 us
  local copies, waits for them, and re-layouts: 2.34 us -> 0.98 us
  waiting for transfers between devices: 15.4 us -> 14.3 us
    unnamed x15 -> x16, local copies, waits for them, and re-layouts: 1.56 us -> 0.03 us
    dot_general x1, matrix products: 3.97 us -> 2.68 us  [body(): jnp.dot(pooled, w_neigh, preferred_element_type=jnp.float32)]
    dot_general x1, matrix products: 1.84 us -> 0.56 us  [body(): lax.dot_general(pick, normed, (((0,), (0,)), ((), ())), preferred_element...]
    dot_general x1, matrix products: 3.06 us -> 2.02 us  [body(): jnp.dot(one_hot(wanted.reshape(-1), row_count), messages, preferred_eleme...]
    dot_general x1, matrix products: 2.48 us -> 3.48 us  [body(): jnp.dot(features, w_self, preferred_element_type=jnp.float32)]
    all_to_all x1, waiting for transfers between devices: 2.81 us -> 1.83 us  [body(): lax.all_to_all(requests.astype(jnp.float32), 'index', split_axis=1, conca...]
    convert_element_type x0 -> x2, other arithmetic: none -> 0.9 us  [the longest x1 0.85 us: body(): requests.astype(jnp.float32)]
  transfers between devices with their start and end apart: 2 -> 2, of which waited for: 2 -> 2; matrix products, arithmetic and copies ran while one was open for 10% -> 12% of each run, Pallas kernels for 0% -> 0%
where the time goes in v6:
time: 80.7 us; the launch traced here: 80.3 us
  blocking collectives  33.3 us (41%)
  starting transfers between devices  14.3 us (18%)
  waiting for transfers between devices  14.3 us (18%)
  matrix products  10.6 us (13%)
  other arithmetic  6.69 us (8%)
  local copies, waits for them, and re-layouts  0.98 us (1%)
    all_to_all x1, blocking collectives, body(): lax.all_to_all(outgoing, 'index', split_axis=0, concat_axis=0, tiled=True)  20.6 us
    all_to_all x1, blocking collectives, body(): lax.all_to_all(raw_scores.reshape(peer_count, arrived.shape[1], cent_coun...  12.7 us
    all_to_all x1, waiting for transfers between devices, body(): lax.all_to_all(outgoing_msgs.reshape(peer_count, fetch_slots, width), 'in...  12.5 us
    all_to_all x1, starting transfers between devices, body(): lax.all_to_all(requests.astype(jnp.float32), 'index', split_axis=1, conca...  8.58 us
    all_to_all x1, starting transfers between devices, body(): lax.all_to_all(outgoing_msgs.reshape(peer_count, fetch_slots, width), 'in...  5.69 us
    reduce_sum x1, other arithmetic, body(): jnp.sum(jnp.where(slots[:, :, None] == slot_ids[None, None, :], weights_n...  4.35 us
    dot_general x1, matrix products, body(): jnp.dot(features, w_self, preferred_element_type=jnp.float32)  3.48 us
    dot_general x1, matrix products, body(): jnp.dot(pooled, w_neigh, preferred_element_type=jnp.float32)  2.68 us
  transfers between devices with their start and end apart: 2, of which 2 were waited for; matrix products, arithmetic and copies ran while one was open for 12% of the time, Pallas kernels for 0%

profile of v6, /device:TPU:1, one launch (start us, length us, event | category | flops | bytes accessed | tf_op | source)
XLA Modules:
  0.0 80.3 jit_solution(5237908899413354754)
XLA Ops:
  0.0 0.0 copy-start
  0.0 0.0 copy-start.7
  0.0 0.8 %convert_element_type.46 = f32[1,32,16]{1,2,0:T(8,128)S(1)} convert(s32[1,32,16]{1,2,0:T(8,128)} %param.18) | non-fusion elementwise | flops 512 | bytes 4096 | tf_op jit(solution)/shard_map/convert_element_type | solution.py:39
  0.9 0.7 copy.23
  1.6 8.6 %all-to-all-start = ((f32[1,32,16]{2,0,1:T(1,128)}), f32[1,32,16]{2,0,1:T(1,128)S(1)}, u32[]{:S(2)}, u32[]{:S(2)}) async-start(f32[1,32,16]{2,0,1:T(1,128)} %copy.23), calls=%async_computation | async-start | bytes 32768 | tf_op jit(solution)/shard_map/all_to_all | solution.py:39
  10.1 0.7 fusion.13
  10.8 0.6 reduce-window.6
  11.4 0.2 slice_reduce_fusion
  11.6 3.5 %fusion.15 = f32[256,1024]{1,0:T(8,128)} fusion(bf16[256,1024]{1,0:T(8,128)(2,1)} %param.11, bf16[1024,1024]{1,0:T(8,128)(2,1)} %param.14), kind=kOutput, calls=%fused_computation.37 | convolution fusion | flops 536870912 | bytes 3670016 | tf_op jit(solution)/shard_map/dot_general | solution.py:62
  15.1 0.0 copy-done.5
  15.1 0.1 fusion.12
  15.2 1.8 %all-to-all-done = f32[1,32,16]{2,0,1:T(1,128)S(1)} async-done(((f32[1,32,16]{2,0,1:T(1,128)}), f32[1,32,16]{2,0,1:T(1,128)S(1)}, u32[]{:S(2)}, u32[]{:S(2)}) %all-to-all-start) | async-done | bytes 2080 | tf_op jit(solution)/shard_map/all_to_all | solution.py:39
  17.0 0.1 convert_reduce_fusion
  17.1 0.1 convert_element_type.48
  17.2 0.0 copy-done
  17.2 0.0 copy-done.1
  17.2 0.0 copy-done.7
  17.2 2.0 %convolution_convert_fusion.1 = bf16[512,1024]{1,0:T(8,128)(2,1)} fusion(bf16[256,1024]{1,0:T(8,128)(2,1)S(1)} %copy-done.1, bf16[1024,1024]{1,0:T(8,128)(2,1)S(1)} %copy-done, f32[1024]{0:T(1024)S(1)} %copy-done.7, s32[512]{0:T(512)S(1)} %convert_element_type.48), kind=kOutput, calls=%fused_computation.3 | convolution fusion | flops 806748160 | bytes 3676160 | tf_op jit(solution)/shard_map/dot_general | solution.py:49
  19.2 5.7 %all-to-all-start.1 = ((bf16[32,16,1024]{2,1,0:T(8,128)(2,1)}), bf16[32,16,1024]{2,1,0:T(8,128)(2,1)S(1)}, u32[]{:S(2)}, u32[]{:S(2)}) async-start(bf16[32,16,1024]{2,1,0:T(8,128)(2,1)} %bitcast.38), calls=%async_computation.1 | async-start | bytes 2097152 | tf_op jit(solution)/shard_map/all_to_all | solution.py:52
  24.9 0.0 copy-done.2
  25.0 0.0 copy-done.3
  25.0 4.3 %select_reduce_fusion = bf16[256,512]{1,0:T(8,128)(2,1)S(1)} fusion(f32[256,50]{0,1:T(8,128)S(1)} %broadcast_divide_fusion, s32[256,50]{0,1:T(8,128)S(1)} %copy-done.3), kind=kLoop, calls=%fused_computation | loop fusion | flops 19529728 | bytes 364544 | tf_op jit(solution)/shard_map/reduce_sum | solution.py:45
  29.4 12.5 %all-to-all-done.1 = bf16[32,16,1024]{2,1,0:T(8,128)(2,1)S(1)} async-done(((bf16[32,16,1024]{2,1,0:T(8,128)(2,1)}), bf16[32,16,1024]{2,1,0:T(8,128)(2,1)S(1)}, u32[]{:S(2)}, u32[]{:S(2)}) %all-to-all-start.1) | async-done | bytes 1048608 | tf_op jit(solution)/shard_map/all_to_all | solution.py:52
  41.8 0.4 convolution_convert_fusion.2
  42.3 0.0 copy-done.4
  42.3 2.7 %multiply_reduce_fusion = (f32[256]{0:T(256)S(1)}, f32[256,1024]{1,0:T(8,128)S(1)}) fusion(f32[1024]{0:T(1024)S(1)} %copy-done.4, f32[256,1024]{1,0:T(8,128)} %fusion.15, bf16[256,1024]{1,0:T(8,128)(2,1)S(1)} %convolution_convert_fusion.2, bf16[1024,1024]{1,0:T(8,128)(2,1)} %param.15), kind=kOutput, calls=%fused_computation.14 | convolution fusion | flops 538181376 | bytes 4723712 | tf_op jit(solution)/shard_map/dot_general | solution.py:63
  45.0 0.0 copy-start.6
  45.0 0.6 convolution_convert_fusion
  45.6 20.6 %all_to_all.20 = bf16[32,16,1024]{2,1,0:T(8,128)(2,1)S(1)} all-to-all(bf16[32,16,1024]{2,1,0:T(8,128)(2,1)S(1)} %bitcast.37), channel_id=1, replica_groups=mesh['graph'=8,'index'=32] {'index'}, dimensions={0} | all-to-all | bytes 2097152 | tf_op jit(solution)/shard_map/all_to_all | solution.py:75
  66.2 0.5 convolution_convert_fusion.3
  66.7 12.7 %all_to_all.21 = bf16[32,16,256]{2,1,0:T(8,128)(2,1)S(1)} all-to-all(bf16[32,16,256]{2,1,0:T(8,128)(2,1)S(1)} %bitcast.41), channel_id=1, replica_groups=mesh['graph'=8,'index'=32] {'index'}, dimensions={0} | all-to-all | bytes 524288 | tf_op jit(solution)/shard_map/all_to_all | solution.py:80
  79.4 0.9 %convolution_convert_fusion.4 = bf16[256,256]{1,0:T(8,128)(2,1)} fusion(bf16[512,256]{1,0:T(8,128)(2,1)S(1)} %bitcast.40, s32[256]{0:T(256)S(1)} %bitcast.45), kind=kOutput, calls=%fused_computation.12 | convolution fusion | flops 67305472 | bytes 394240 | tf_op jit(solution)/shard_map/dot_general | solution.py:87
  (12 shorter events, 0.1 us)
Async XLA Ops:
  0.0 17.2 %copy-start = (bf16[1024,1024]{1,0:T(8,128)(2,1)S(1)}, bf16[1024,1024]{1,0:T(8,128)(2,1)}, u32[]{:S(2)}) copy-start(bf16[1024,1024]{1,0:T(8,128)(2,1)} %param.12) | copy-start | bytes 6291460
  0.0 15.1 %copy-start.5 = (s32[256,1]{0,1:T(1,128)S(1)}, s32[256,1]{0,1:T(1,128)}, u32[]{:S(2)}) copy-start(s32[256,1]{0,1:T(1,128)} %param.21) | copy-start | bytes 3076
  0.0 17.2 %copy-start.1 = (bf16[256,1024]{1,0:T(8,128)(2,1)S(1)}, bf16[256,1024]{1,0:T(8,128)(2,1)}, u32[]{:S(2)}) copy-start(bf16[256,1024]{1,0:T(8,128)(2,1)} %param.11) | copy-start | bytes 1572868
  0.0 17.2 %copy-start.7 = (f32[1024]{0:T(1024)S(1)}, f32[1024]{0:T(1024)}, u32[]{:S(2)}) copy-start(f32[1024]{0:T(1024)} %param.13) | copy-start | bytes 12292
  1.6 15.5 %all-to-all-start = ((f32[1,32,16]{2,0,1:T(1,128)}), f32[1,32,16]{2,0,1:T(1,128)S(1)}, u32[]{:S(2)}, u32[]{:S(2)}) async-start(f32[1,32,16]{2,0,1:T(1,128)} %copy.23), calls=%async_computation | async-start | bytes 32768 | tf_op jit(solution)/shard_map/all_to_all | solution.py:39
  19.2 5.7 %copy-start.2 = (f32[256,50]{0,1:T(8,128)S(1)}, f32[256,50]{0,1:T(8,128)}, u32[]{:S(2)}) copy-start(f32[256,50]{0,1:T(8,128)} %param.20) | copy-start | bytes 153604
  19.2 5.8 %copy-start.3 = (s32[256,50]{0,1:T(8,128)S(1)}, s32[256,50]{0,1:T(8,128)}, u32[]{:S(2)}) copy-start(s32[256,50]{0,1:T(8,128)} %param.19) | copy-start | bytes 153604
  19.2 23.1 %copy-start.4 = (f32[1024]{0:T(1024)S(1)}, f32[1024]{0:T(1024)}, u32[]{:S(2)}) copy-start(f32[1024]{0:T(1024)} %param.16) | copy-start | bytes 12292
  19.2 22.6 %all-to-all-start.1 = ((bf16[32,16,1024]{2,1,0:T(8,128)(2,1)}), bf16[32,16,1024]{2,1,0:T(8,128)(2,1)S(1)}, u32[]{:S(2)}, u32[]{:S(2)}) async-start(bf16[32,16,1024]{2,1,0:T(8,128)(2,1)} %bitcast.38), calls=%async_computation.1 | async-start | bytes 2097152 | tf_op jit(solution)/shard_map/all_to_all | solution.py:52
  45.0 21.2 %copy-start.6 = (bf16[256,1024]{1,0:T(8,128)(2,1)S(1)}, bf16[256,1024]{1,0:T(8,128)(2,1)}, u32[]{:S(2)}) copy-start(bf16[256,1024]{1,0:T(8,128)(2,1)} %param.17) | copy-start | bytes 1572868

commit v7 on v6

--- a/solution.py
+++ b/solution.py
@@ -47,7 +47,9 @@
         axis=1,
     ).astype(jnp.bfloat16)
     outgoing_msgs = jnp.dot(
-        one_hot(wanted.reshape(-1), row_count), messages, preferred_element_type=jnp.float32
+        one_hot(wanted.reshape(-1), row_count),
+        lax.optimization_barrier(messages),
+        preferred_element_type=jnp.float32,
     ).astype(jnp.bfloat16)
     fetched = lax.all_to_all(
         outgoing_msgs.reshape(peer_count, fetch_slots, width),

time: 80.7 us -> 80.5 us (level)
  waiting for transfers between devices: 14.3 us -> 13.4 us
  starting transfers between devices: 14.3 us -> 15.2 us
    all_to_all x1, starting transfers between devices: 5.69 us -> 6.6 us  [body(): lax.all_to_all(outgoing_msgs.reshape(peer_count, fetch_slots, width), 'in...]
    all_to_all x1, waiting for transfers between devices: 1.83 us -> 0.93 us  [body(): lax.all_to_all(requests.astype(jnp.float32), 'index', split_axis=1, conca...]
    dot_general x1 -> x2, matrix products: 2.02 us -> 2.23 us  [the longest x1 1.52 us: body(): jnp.dot(one_hot(wanted.reshape(-1), row_count), lax.optimization_barrier(...]
  transfers between devices with their start and end apart: 2 -> 2, of which waited for: 2 -> 2; matrix products, arithmetic and copies ran while one was open for 12% -> 13% of each run, Pallas kernels for 0% -> 0%
where the time goes in v7:
time: 80.5 us; the launch traced here: 80.1 us
  blocking collectives  33.3 us (41%)
  starting transfers between devices  15.2 us (19%)
  waiting for transfers between devices  13.4 us (17%)
  matrix products  10.3 us (13%)
  other arithmetic  6.69 us (8%)
  local copies, waits for them, and re-layouts  0.99 us (1%)
    all_to_all x1, blocking collectives, body(): lax.all_to_all(outgoing, 'index', split_axis=0, concat_axis=0, tiled=True)  20.6 us
    all_to_all x1, blocking collectives, body(): lax.all_to_all(raw_scores.reshape(peer_count, arrived.shape[1], cent_coun...  12.7 us
    all_to_all x1, waiting for transfers between devices, body(): lax.all_to_all(outgoing_msgs.reshape(peer_count, fetch_slots, width), 'in...  12.5 us
    all_to_all x1, starting transfers between devices, body(): lax.all_to_all(requests.astype(jnp.float32), 'index', split_axis=1, conca...  8.58 us
    all_to_all x1, starting transfers between devices, body(): lax.all_to_all(outgoing_msgs.reshape(peer_count, fetch_slots, width), 'in...  6.6 us
    reduce_sum x1, other arithmetic, body(): jnp.sum(jnp.where(slots[:, :, None] == slot_ids[None, None, :], weights_n...  4.35 us
    dot_general x1, matrix products, body(): jnp.dot(features, w_self, preferred_element_type=jnp.float32)  3.61 us
    dot_general x1, matrix products, body(): jnp.dot(pooled, w_neigh, preferred_element_type=jnp.float32)  2.05 us
  transfers between devices with their start and end apart: 2, of which 2 were waited for; matrix products, arithmetic and copies ran while one was open for 13% of the time, Pallas kernels for 0%

profile of v7, /device:TPU:1, one launch (start us, length us, event | category | flops | bytes accessed | tf_op | source)
XLA Modules:
  0.0 80.1 jit_solution(9399820236700699019)
XLA Ops:
  0.0 0.0 copy-start
  0.0 0.8 %convert_element_type.46 = f32[1,32,16]{1,2,0:T(8,128)S(1)} convert(s32[1,32,16]{1,2,0:T(8,128)} %param.18) | non-fusion elementwise | flops 512 | bytes 4096 | tf_op jit(solution)/shard_map/convert_element_type | solution.py:39
  0.9 0.7 copy.23
  1.5 8.6 %all-to-all-start = ((f32[1,32,16]{2,0,1:T(1,128)}), f32[1,32,16]{2,0,1:T(1,128)S(1)}, u32[]{:S(2)}, u32[]{:S(2)}) async-start(f32[1,32,16]{2,0,1:T(1,128)} %copy.23), calls=%async_computation | async-start | bytes 32768 | tf_op jit(solution)/shard_map/all_to_all | solution.py:39
  10.1 0.7 fusion.11
  10.8 0.6 reduce-window.6
  11.4 0.2 slice_reduce_fusion
  11.6 3.6 %fusion.12 = f32[256,1024]{1,0:T(8,128)} fusion(bf16[256,1024]{1,0:T(8,128)(2,1)} %param.11, bf16[1024,1024]{1,0:T(8,128)(2,1)} %param.14), kind=kOutput, calls=%fused_computation.34 | convolution fusion | flops 536870912 | bytes 3670016 | tf_op jit(solution)/shard_map/dot_general | solution.py:64
  15.2 0.0 copy-done.1
  15.2 0.0 copy-done.8
  15.2 0.0 copy-done.6
  15.2 0.0 copy-start.5
  15.2 0.7 fusion.3
  16.0 0.0 copy-start.2
  16.0 0.0 copy-start.3
  16.0 0.0 copy-done.5
  16.0 0.1 fusion.10
  16.1 0.9 %all-to-all-done = f32[1,32,16]{2,0,1:T(1,128)S(1)} async-done(((f32[1,32,16]{2,0,1:T(1,128)}), f32[1,32,16]{2,0,1:T(1,128)S(1)}, u32[]{:S(2)}, u32[]{:S(2)}) %all-to-all-start) | async-done | bytes 2080 | tf_op jit(solution)/shard_map/all_to_all | solution.py:39
  17.0 0.1 convert_reduce_fusion
  17.1 0.1 convert_element_type.48
  17.2 1.5 %convolution_convert_fusion.1 = bf16[512,1024]{1,0:T(8,128)(2,1)} fusion(bf16[256,1024]{1,0:T(8,128)(2,1)S(1)} %fusion.3, s32[512]{0:T(512)S(1)} %convert_element_type.48), kind=kOutput, calls=%fused_computation.3 | convolution fusion | flops 269090816 | bytes 1574912 | tf_op jit(solution)/shard_map/dot_general | solution.py:49
  18.7 6.6 %all-to-all-start.1 = ((bf16[32,16,1024]{2,1,0:T(8,128)(2,1)}), bf16[32,16,1024]{2,1,0:T(8,128)(2,1)S(1)}, u32[]{:S(2)}, u32[]{:S(2)}) async-start(bf16[32,16,1024]{2,1,0:T(8,128)(2,1)} %bitcast.39), calls=%async_computation.1 | async-start | bytes 2097152 | tf_op jit(solution)/shard_map/all_to_all | solution.py:54
  25.4 4.3 %select_reduce_fusion = bf16[256,512]{1,0:T(8,128)(2,1)S(1)} fusion(f32[256,50]{0,1:T(8,128)S(1)} %broadcast_divide_fusion, s32[256,50]{0,1:T(8,128)S(1)} %copy-done.3), kind=kLoop, calls=%fused_computation | loop fusion | flops 19529728 | bytes 364544 | tf_op jit(solution)/shard_map/reduce_sum | solution.py:45
  29.7 12.5 %all-to-all-done.1 = bf16[32,16,1024]{2,1,0:T(8,128)(2,1)S(1)} async-done(((bf16[32,16,1024]{2,1,0:T(8,128)(2,1)}), bf16[32,16,1024]{2,1,0:T(8,128)(2,1)S(1)}, u32[]{:S(2)}, u32[]{:S(2)}) %all-to-all-start.1) | async-done | bytes 1048608 | tf_op jit(solution)/shard_map/all_to_all | solution.py:54
  42.2 0.4 convolution_convert_fusion.2
  42.7 2.1 %multiply_reduce_fusion = (f32[256]{0:T(256)S(1)}, f32[256,1024]{1,0:T(8,128)S(1)}) fusion(f32[1024]{0:T(1024)S(1)} %copy-done.4, f32[256,1024]{1,0:T(8,128)} %fusion.12, bf16[256,1024]{1,0:T(8,128)(2,1)S(1)} %convolution_convert_fusion.2, bf16[1024,1024]{1,0:T(8,128)(2,1)S(1)} %copy-done), kind=kOutput, calls=%fused_computation.14 | convolution fusion | flops 538181376 | bytes 4723712 | tf_op jit(solution)/shard_map/dot_general | solution.py:65
  44.7 0.0 copy-start.7
  44.7 0.6 convolution_convert_fusion
  45.3 20.6 %all_to_all.20 = bf16[32,16,1024]{2,1,0:T(8,128)(2,1)S(1)} all-to-all(bf16[32,16,1024]{2,1,0:T(8,128)(2,1)S(1)} %bitcast.38), channel_id=1, replica_groups=mesh['graph'=8,'index'=32] {'index'}, dimensions={0} | all-to-all | bytes 2097152 | tf_op jit(solution)/shard_map/all_to_all | solution.py:77
  65.9 0.5 convolution_convert_fusion.3
  66.4 12.7 %all_to_all.21 = bf16[32,16,256]{2,1,0:T(8,128)(2,1)S(1)} all-to-all(bf16[32,16,256]{2,1,0:T(8,128)(2,1)S(1)} %bitcast.42), channel_id=1, replica_groups=mesh['graph'=8,'index'=32] {'index'}, dimensions={0} | all-to-all | bytes 524288 | tf_op jit(solution)/shard_map/all_to_all | solution.py:82
  79.1 0.9 %convolution_convert_fusion.4 = bf16[256,256]{1,0:T(8,128)(2,1)} fusion(bf16[512,256]{1,0:T(8,128)(2,1)S(1)} %bitcast.41, s32[256]{0:T(256)S(1)} %bitcast.46), kind=kOutput, calls=%fused_computation.12 | convolution fusion | flops 67305472 | bytes 394240 | tf_op jit(solution)/shard_map/dot_general | solution.py:89
  (15 shorter events, 0.1 us)
Async XLA Ops:
  0.0 42.6 %copy-start = (bf16[1024,1024]{1,0:T(8,128)(2,1)S(1)}, bf16[1024,1024]{1,0:T(8,128)(2,1)}, u32[]{:S(2)}) copy-start(bf16[1024,1024]{1,0:T(8,128)(2,1)} %param.15) | copy-start | bytes 6291460
  0.0 15.2 %copy-start.1 = (bf16[256,1024]{1,0:T(8,128)(2,1)S(1)}, bf16[256,1024]{1,0:T(8,128)(2,1)}, u32[]{:S(2)}) copy-start(bf16[256,1024]{1,0:T(8,128)(2,1)} %param.11) | copy-start | bytes 1572868
  0.0 15.2 %copy-start.8 = (f32[1024]{0:T(1024)S(1)}, f32[1024]{0:T(1024)}, u32[]{:S(2)}) copy-start(f32[1024]{0:T(1024)} %param.13) | copy-start | bytes 12292
  1.5 15.5 %all-to-all-start = ((f32[1,32,16]{2,0,1:T(1,128)}), f32[1,32,16]{2,0,1:T(1,128)S(1)}, u32[]{:S(2)}, u32[]{:S(2)}) async-start(f32[1,32,16]{2,0,1:T(1,128)} %copy.23), calls=%async_computation | async-start | bytes 32768 | tf_op jit(solution)/shard_map/all_to_all | solution.py:39
  11.6 3.6 %copy-start.6 = (bf16[1024,1024]{1,0:T(8,128)(2,1)S(1)}, bf16[1024,1024]{1,0:T(8,128)(2,1)}, u32[]{:S(2)}) copy-start(bf16[1024,1024]{1,0:T(8,128)(2,1)} %param.12) | copy-start | bytes 6291460
  15.2 0.8 copy-start.5
  16.0 9.3 %copy-start.2 = (f32[256,50]{0,1:T(8,128)S(1)}, f32[256,50]{0,1:T(8,128)}, u32[]{:S(2)}) copy-start(f32[256,50]{0,1:T(8,128)} %param.20) | copy-start | bytes 153604
  16.0 9.4 %copy-start.3 = (s32[256,50]{0,1:T(8,128)S(1)}, s32[256,50]{0,1:T(8,128)}, u32[]{:S(2)}) copy-start(s32[256,50]{0,1:T(8,128)} %param.19) | copy-start | bytes 153604
  18.7 24.0 %copy-start.4 = (f32[1024]{0:T(1024)S(1)}, f32[1024]{0:T(1024)}, u32[]{:S(2)}) copy-start(f32[1024]{0:T(1024)} %param.16) | copy-start | bytes 12292
  18.7 23.5 %all-to-all-start.1 = ((bf16[32,16,1024]{2,1,0:T(8,128)(2,1)}), bf16[32,16,1024]{2,1,0:T(8,128)(2,1)S(1)}, u32[]{:S(2)}, u32[]{:S(2)}) async-start(bf16[32,16,1024]{2,1,0:T(8,128)(2,1)} %bitcast.39), calls=%async_computation.1 | async-start | bytes 2097152 | tf_op jit(solution)/shard_map/all_to_all | solution.py:54
  44.7 21.2 %copy-start.7 = (bf16[256,1024]{1,0:T(8,128)(2,1)S(1)}, bf16[256,1024]{1,0:T(8,128)(2,1)}, u32[]{:S(2)}) copy-start(bf16[256,1024]{1,0:T(8,128)(2,1)} %param.17) | copy-start | bytes 1572868

commit v8 on v7

--- a/solution.py
+++ b/solution.py
@@ -36,7 +36,9 @@
     fetch_slots = requests.shape[2]
     slot_count = peer_count * fetch_slots
     cent_count = centroids.shape[0]
-    wanted = lax.all_to_all(requests.astype(jnp.float32), "index", split_axis=1, concat_axis=1, tiled=True)[0].astype(jnp.int32)
+    peer_eye = jnp.eye(peer_count, dtype=jnp.bfloat16)
+    asked = jnp.dot(peer_eye, requests[0].astype(jnp.bfloat16), preferred_element_type=jnp.float32)
+    wanted = lax.all_to_all(asked, "index", split_axis=0, concat_axis=0, tiled=True).astype(jnp.int32)
     messages = jax.nn.relu(
         jnp.dot(features, q_weight, preferred_element_type=jnp.float32) + q_bias
     ).astype(jnp.bfloat16)

time: 80.5 us -> 80.5 us (level)
  matrix products: 10.3 us -> 11.9 us
  other arithmetic: 6.69 us -> 5.84 us
    dot_general x0 -> x1, matrix products: none -> 1.57 us  [body(): jnp.dot(peer_eye, requests[0].astype(jnp.bfloat16), preferred_element_typ...]
    convert_element_type x2 -> x1, other arithmetic: 0.9 us -> 0.05 us  [body(): lax.all_to_all(asked, 'index', split_axis=0, concat_axis=0, tiled=True)]
where the time goes in v8:
time: 80.5 us; the launch traced here: 80.1 us
  blocking collectives  33.3 us (41%)
  starting transfers between devices  15.2 us (19%)
  waiting for transfers between devices  13.4 us (17%)
  matrix products  11.9 us (15%)
  other arithmetic  5.84 us (7%)
    all_to_all x1, blocking collectives, body(): lax.all_to_all(outgoing, 'index', split_axis=0, concat_axis=0, tiled=True)  20.6 us
    all_to_all x1, blocking collectives, body(): lax.all_to_all(raw_scores.reshape(peer_count, arrived.shape[1], cent_coun...  12.7 us
    all_to_all x1, waiting for transfers between devices, body(): lax.all_to_all(outgoing_msgs.reshape(peer_count, fetch_slots, width), 'in...  12.5 us
    all_to_all x1, starting transfers between devices, body(): lax.all_to_all(asked, 'index', split_axis=0, concat_axis=0, tiled=True)  8.58 us
    all_to_all x1, starting transfers between devices, body(): lax.all_to_all(outgoing_msgs.reshape(peer_count, fetch_slots, width), 'in...  6.59 us
    reduce_sum x1, other arithmetic, body(): jnp.sum(jnp.where(slots[:, :, None] == slot_ids[None, None, :], weights_n...  4.35 us
    dot_general x1, matrix products, body(): jnp.dot(features, w_self, preferred_element_type=jnp.float32)  3.61 us
    dot_general x1, matrix products, body(): jnp.dot(pooled, w_neigh, preferred_element_type=jnp.float32)  2.05 us
  transfers between devices with their start and end apart: 2, of which 2 were waited for; matrix products, arithmetic and copies ran while one was open for 13% of the time, Pallas kernels for 0%

profile of v8, /device:TPU:1, one launch (start us, length us, event | category | flops | bytes accessed | tf_op | source)
XLA Modules:
  0.0 80.1 jit_solution(8922668098141098397)
XLA Ops:
  0.0 0.0 copy-start
  0.0 1.6 %fusion.12 = f32[32,16]{1,0:T(8,128)} fusion(s32[1,32,16]{1,2,0:T(8,128)} %param.18), kind=kOutput, calls=%fused_computation.33 | convolution fusion | flops 34304 | bytes 4096 | tf_op jit(solution)/shard_map/dot_general | solution.py:40
  1.6 8.6 %all-to-all-start = ((f32[32,1,16]{2,1,0:T(1,128)}), f32[32,1,16]{2,1,0:T(1,128)S(1)}, u32[]{:S(2)}, u32[]{:S(2)}) async-start(f32[32,1,16]{2,1,0:T(1,128)} %bitcast.13), calls=%async_computation | async-start | bytes 32768 | tf_op jit(solution)/shard_map/all_to_all | solution.py:41
  10.2 0.7 fusion.11
  10.9 0.6 reduce-window.6
  11.4 0.2 slice_reduce_fusion
  11.7 3.6 %fusion.15 = f32[256,1024]{1,0:T(8,128)} fusion(bf16[256,1024]{1,0:T(8,128)(2,1)} %param.11, bf16[1024,1024]{1,0:T(8,128)(2,1)} %param.14), kind=kOutput, calls=%fused_computation.38 | convolution fusion | flops 536870912 | bytes 3670016 | tf_op jit(solution)/shard_map/dot_general | solution.py:66
  15.3 0.0 copy-done.1
  15.3 0.0 copy-done.8
  15.3 0.0 copy-done.6
  15.3 0.0 copy-start.5
  15.3 0.7 fusion.3
  16.0 0.0 copy-start.2
  16.0 0.0 copy-start.3
  16.0 0.0 copy-done.5
  16.0 0.1 fusion.10
  16.1 0.9 %all-to-all-done = f32[32,1,16]{2,1,0:T(1,128)S(1)} async-done(((f32[32,1,16]{2,1,0:T(1,128)}), f32[32,1,16]{2,1,0:T(1,128)S(1)}, u32[]{:S(2)}, u32[]{:S(2)}) %all-to-all-start) | async-done | bytes 2080 | tf_op jit(solution)/shard_map/all_to_all | solution.py:41
  17.1 0.1 convert_reduce_fusion
  17.1 0.1 convert_element_type.53
  17.2 1.5 %convolution_convert_fusion.1 = bf16[512,1024]{1,0:T(8,128)(2,1)} fusion(bf16[256,1024]{1,0:T(8,128)(2,1)S(1)} %fusion.3, s32[512]{0:T(512)S(1)} %convert_element_type.53), kind=kOutput, calls=%fused_computation.3 | convolution fusion | flops 269090816 | bytes 1574912 | tf_op jit(solution)/shard_map/dot_general | solution.py:51
  18.7 6.6 %all-to-all-start.1 = ((bf16[32,16,1024]{2,1,0:T(8,128)(2,1)}), bf16[32,16,1024]{2,1,0:T(8,128)(2,1)S(1)}, u32[]{:S(2)}, u32[]{:S(2)}) async-start(bf16[32,16,1024]{2,1,0:T(8,128)(2,1)} %bitcast.44), calls=%async_computation.1 | async-start | bytes 2097152 | tf_op jit(solution)/shard_map/all_to_all | solution.py:56
  25.4 0.0 copy-done.3
  25.4 4.3 %select_reduce_fusion = bf16[256,512]{1,0:T(8,128)(2,1)S(1)} fusion(f32[256,50]{0,1:T(8,128)S(1)} %broadcast_divide_fusion, s32[256,50]{0,1:T(8,128)S(1)} %copy-done.3), kind=kLoop, calls=%fused_computation | loop fusion | flops 19529728 | bytes 364544 | tf_op jit(solution)/shard_map/reduce_sum | solution.py:47
  29.8 12.5 %all-to-all-done.1 = bf16[32,16,1024]{2,1,0:T(8,128)(2,1)S(1)} async-done(((bf16[32,16,1024]{2,1,0:T(8,128)(2,1)}), bf16[32,16,1024]{2,1,0:T(8,128)(2,1)S(1)}, u32[]{:S(2)}, u32[]{:S(2)}) %all-to-all-start.1) | async-done | bytes 1048608 | tf_op jit(solution)/shard_map/all_to_all | solution.py:56
  42.2 0.4 convolution_convert_fusion.2
  42.7 2.1 %multiply_reduce_fusion = (f32[256]{0:T(256)S(1)}, f32[256,1024]{1,0:T(8,128)S(1)}) fusion(f32[1024]{0:T(1024)S(1)} %copy-done.4, f32[256,1024]{1,0:T(8,128)} %fusion.15, bf16[256,1024]{1,0:T(8,128)(2,1)S(1)} %convolution_convert_fusion.2, bf16[1024,1024]{1,0:T(8,128)(2,1)S(1)} %copy-done), kind=kOutput, calls=%fused_computation.14 | convolution fusion | flops 538181376 | bytes 4723712 | tf_op jit(solution)/shard_map/dot_general | solution.py:67
  44.8 0.0 copy-start.7
  44.8 0.6 convolution_convert_fusion
  45.4 20.6 %all_to_all.24 = bf16[32,16,1024]{2,1,0:T(8,128)(2,1)S(1)} all-to-all(bf16[32,16,1024]{2,1,0:T(8,128)(2,1)S(1)} %bitcast.43), channel_id=1, replica_groups=mesh['graph'=8,'index'=32] {'index'}, dimensions={0} | all-to-all | bytes 2097152 | tf_op jit(solution)/shard_map/all_to_all | solution.py:79
  66.0 0.5 convolution_convert_fusion.3
  66.5 12.7 %all_to_all.25 = bf16[32,16,256]{2,1,0:T(8,128)(2,1)S(1)} all-to-all(bf16[32,16,256]{2,1,0:T(8,128)(2,1)S(1)} %bitcast.47), channel_id=1, replica_groups=mesh['graph'=8,'index'=32] {'index'}, dimensions={0} | all-to-all | bytes 524288 | tf_op jit(solution)/shard_map/all_to_all | solution.py:84
  79.2 0.9 %convolution_convert_fusion.4 = bf16[256,256]{1,0:T(8,128)(2,1)} fusion(bf16[512,256]{1,0:T(8,128)(2,1)S(1)} %bitcast.46, s32[256]{0:T(256)S(1)} %bitcast.51), kind=kOutput, calls=%fused_computation.12 | convolution fusion | flops 67305472 | bytes 394240 | tf_op jit(solution)/shard_map/dot_general | solution.py:91
  (14 shorter events, 0.1 us)
Async XLA Ops:
  0.0 42.7 %copy-start = (bf16[1024,1024]{1,0:T(8,128)(2,1)S(1)}, bf16[1024,1024]{1,0:T(8,128)(2,1)}, u32[]{:S(2)}) copy-start(bf16[1024,1024]{1,0:T(8,128)(2,1)} %param.15) | copy-start | bytes 6291460
  0.0 15.3 %copy-start.1 = (bf16[256,1024]{1,0:T(8,128)(2,1)S(1)}, bf16[256,1024]{1,0:T(8,128)(2,1)}, u32[]{:S(2)}) copy-start(bf16[256,1024]{1,0:T(8,128)(2,1)} %param.11) | copy-start | bytes 1572868
  0.0 15.3 %copy-start.8 = (f32[1024]{0:T(1024)S(1)}, f32[1024]{0:T(1024)}, u32[]{:S(2)}) copy-start(f32[1024]{0:T(1024)} %param.13) | copy-start | bytes 12292
  1.6 15.5 %all-to-all-start = ((f32[32,1,16]{2,1,0:T(1,128)}), f32[32,1,16]{2,1,0:T(1,128)S(1)}, u32[]{:S(2)}, u32[]{:S(2)}) async-start(f32[32,1,16]{2,1,0:T(1,128)} %bitcast.13), calls=%async_computation | async-start | bytes 32768 | tf_op jit(solution)/shard_map/all_to_all | solution.py:41
  11.7 3.6 %copy-start.6 = (bf16[1024,1024]{1,0:T(8,128)(2,1)S(1)}, bf16[1024,1024]{1,0:T(8,128)(2,1)}, u32[]{:S(2)}) copy-start(bf16[1024,1024]{1,0:T(8,128)(2,1)} %param.12) | copy-start | bytes 6291460
  15.3 0.8 copy-start.5
  16.0 9.3 %copy-start.2 = (f32[256,50]{0,1:T(8,128)S(1)}, f32[256,50]{0,1:T(8,128)}, u32[]{:S(2)}) copy-start(f32[256,50]{0,1:T(8,128)} %param.20) | copy-start | bytes 153604
  16.0 9.4 %copy-start.3 = (s32[256,50]{0,1:T(8,128)S(1)}, s32[256,50]{0,1:T(8,128)}, u32[]{:S(2)}) copy-start(s32[256,50]{0,1:T(8,128)} %param.19) | copy-start | bytes 153604
  18.7 24.0 %copy-start.4 = (f32[1024]{0:T(1024)S(1)}, f32[1024]{0:T(1024)}, u32[]{:S(2)}) copy-start(f32[1024]{0:T(1024)} %param.16) | copy-start | bytes 12292
  18.7 23.5 %all-to-all-start.1 = ((bf16[32,16,1024]{2,1,0:T(8,128)(2,1)}), bf16[32,16,1024]{2,1,0:T(8,128)(2,1)S(1)}, u32[]{:S(2)}, u32[]{:S(2)}) async-start(bf16[32,16,1024]{2,1,0:T(8,128)(2,1)} %bitcast.44), calls=%async_computation.1 | async-start | bytes 2097152 | tf_op jit(solution)/shard_map/all_to_all | solution.py:56
  44.8 21.2 %copy-start.7 = (bf16[256,1024]{1,0:T(8,128)(2,1)S(1)}, bf16[256,1024]{1,0:T(8,128)(2,1)}, u32[]{:S(2)}) copy-start(bf16[256,1024]{1,0:T(8,128)(2,1)} %param.17) | copy-start | bytes 1572868

commit v9 on v8

--- a/solution.py
+++ b/solution.py
@@ -38,7 +38,7 @@
     cent_count = centroids.shape[0]
     peer_eye = jnp.eye(peer_count, dtype=jnp.bfloat16)
     asked = jnp.dot(peer_eye, requests[0].astype(jnp.bfloat16), preferred_element_type=jnp.float32)
-    wanted = lax.all_to_all(asked, "index", split_axis=0, concat_axis=0, tiled=True).astype(jnp.int32)
+    wanted = lax.all_to_all(asked, "index", split_axis=0, concat_axis=0, tiled=True)
     messages = jax.nn.relu(
         jnp.dot(features, q_weight, preferred_element_type=jnp.float32) + q_bias
     ).astype(jnp.bfloat16)
@@ -49,7 +49,9 @@
         axis=1,
     ).astype(jnp.bfloat16)
     outgoing_msgs = jnp.dot(
-        one_hot(wanted.reshape(-1), row_count),
+        (wanted.reshape(-1)[:, None] == jnp.arange(row_count, dtype=jnp.float32)[None, :]).astype(
+            jnp.bfloat16
+        ),
         lax.optimization_barrier(messages),
         preferred_element_type=jnp.float32,
     ).astype(jnp.bfloat16)

time: 80.5 us -> 81.7 us (1.015)
  no operation moved by 1% of the time
where the time goes in v9:
time: 81.7 us; the launch traced here: 81.2 us
  blocking collectives  33.3 us (41%)
  starting transfers between devices  15.2 us (19%)
  waiting for transfers between devices  13.4 us (16%)
  matrix products  11.9 us (15%)
  other arithmetic  6.47 us (8%)
  local copies, waits for them, and re-layouts  0.82 us (1%)
    all_to_all x1, blocking collectives, body(): lax.all_to_all(outgoing, 'index', split_axis=0, concat_axis=0, tiled=True)  20.6 us
    all_to_all x1, blocking collectives, body(): lax.all_to_all(raw_scores.reshape(peer_count, arrived.shape[1], cent_coun...  12.7 us
    all_to_all x1, waiting for transfers between devices, body(): lax.all_to_all(outgoing_msgs.reshape(peer_count, fetch_slots, width), 'in...  12.5 us
    all_to_all x1, starting transfers between devices, body(): lax.all_to_all(asked, 'index', split_axis=0, concat_axis=0, tiled=True)  8.58 us
    all_to_all x1, starting transfers between devices, body(): lax.all_to_all(outgoing_msgs.reshape(peer_count, fetch_slots, width), 'in...  6.59 us
    reduce_sum x1, other arithmetic, body(): jnp.sum(jnp.where(slots[:, :, None] == slot_ids[None, None, :], weights_n...  4.35 us
    dot_general x1, matrix products, body(): jnp.dot(features, w_self, preferred_element_type=jnp.float32)  3.61 us
    dot_general x1, matrix products, body(): jnp.dot(pooled, w_neigh, preferred_element_type=jnp.float32)  2.05 us
  transfers between devices with their start and end apart: 2, of which 2 were waited for; matrix products, arithmetic and copies ran while one was open for 13% of the time, Pallas kernels for 0%

profile of v9, /device:TPU:1, one launch (start us, length us, event | category | flops | bytes accessed | tf_op | source)
XLA Modules:
  0.0 81.2 jit_solution(13401450851866045828)
XLA Ops:
  0.0 0.0 copy-start
  0.0 1.6 %fusion.12 = f32[32,16]{1,0:T(8,128)} fusion(s32[1,32,16]{1,2,0:T(8,128)} %param.18), kind=kOutput, calls=%fused_computation.32 | convolution fusion | flops 34304 | bytes 4096 | tf_op jit(solution)/shard_map/dot_general | solution.py:40
  1.6 8.6 %all-to-all-start = ((f32[32,1,16]{2,1,0:T(1,128)}), f32[32,1,16]{2,1,0:T(1,128)S(1)}, u32[]{:S(2)}, u32[]{:S(2)}) async-start(f32[32,1,16]{2,1,0:T(1,128)} %bitcast.13), calls=%async_computation | async-start | bytes 32768 | tf_op jit(solution)/shard_map/all_to_all | solution.py:41
  10.2 0.7 fusion.11
  10.9 0.6 reduce-window.6
  11.4 0.2 slice_reduce_fusion
  11.7 3.6 %fusion.15 = f32[256,1024]{1,0:T(8,128)} fusion(bf16[256,1024]{1,0:T(8,128)(2,1)} %param.11, bf16[1024,1024]{1,0:T(8,128)(2,1)} %param.14), kind=kOutput, calls=%fused_computation.37 | convolution fusion | flops 536870912 | bytes 3670016 | tf_op jit(solution)/shard_map/dot_general | solution.py:68
  15.3 0.0 copy-done.1
  15.3 0.0 copy-done.8
  15.3 0.0 copy-done.6
  15.3 0.0 copy-start.5
  15.3 0.7 fusion.3
  16.0 0.0 copy-start.2
  16.0 0.0 copy-start.3
  16.0 0.0 copy-done.5
  16.0 0.1 fusion.10
  16.1 0.9 %all-to-all-done = f32[32,1,16]{2,1,0:T(1,128)S(1)} async-done(((f32[32,1,16]{2,1,0:T(1,128)}), f32[32,1,16]{2,1,0:T(1,128)S(1)}, u32[]{:S(2)}, u32[]{:S(2)}) %all-to-all-start) | async-done | bytes 2080 | tf_op jit(solution)/shard_map/all_to_all | solution.py:41
  17.1 0.5 broadcast.48
  17.6 0.7 reduce.5
  18.3 0.1 eq.87
  18.4 1.5 %convolution_convert_fusion.1 = bf16[512,1024]{1,0:T(8,128)(2,1)} fusion(bf16[256,1024]{1,0:T(8,128)(2,1)S(1)} %fusion.3, f32[512]{0:T(512)S(1)} %eq.87), kind=kOutput, calls=%fused_computation.3 | convolution fusion | flops 269090816 | bytes 1574912 | tf_op jit(solution)/shard_map/dot_general | solution.py:51
  19.9 6.6 %all-to-all-start.1 = ((bf16[32,16,1024]{2,1,0:T(8,128)(2,1)}), bf16[32,16,1024]{2,1,0:T(8,128)(2,1)S(1)}, u32[]{:S(2)}, u32[]{:S(2)}) async-start(bf16[32,16,1024]{2,1,0:T(8,128)(2,1)} %bitcast.44), calls=%async_computation.1 | async-start | bytes 2097152 | tf_op jit(solution)/shard_map/all_to_all | solution.py:58
  26.6 4.3 %select_reduce_fusion = bf16[256,512]{1,0:T(8,128)(2,1)S(1)} fusion(f32[256,50]{0,1:T(8,128)S(1)} %broadcast_divide_fusion, s32[256,50]{0,1:T(8,128)S(1)} %copy-done.3), kind=kLoop, calls=%fused_computation | loop fusion | flops 19529728 | bytes 364544 | tf_op jit(solution)/shard_map/reduce_sum | solution.py:47
  30.9 12.5 %all-to-all-done.1 = bf16[32,16,1024]{2,1,0:T(8,128)(2,1)S(1)} async-done(((bf16[32,16,1024]{2,1,0:T(8,128)(2,1)}), bf16[32,16,1024]{2,1,0:T(8,128)(2,1)S(1)}, u32[]{:S(2)}, u32[]{:S(2)}) %all-to-all-start.1) | async-done | bytes 1048608 | tf_op jit(solution)/shard_map/all_to_all | solution.py:58
  43.4 0.4 convolution_convert_fusion.2
  43.9 2.1 %multiply_reduce_fusion = (f32[256]{0:T(256)S(1)}, f32[256,1024]{1,0:T(8,128)S(1)}) fusion(f32[1024]{0:T(1024)S(1)} %copy-done.4, f32[256,1024]{1,0:T(8,128)} %fusion.15, bf16[256,1024]{1,0:T(8,128)(2,1)S(1)} %convolution_convert_fusion.2, bf16[1024,1024]{1,0:T(8,128)(2,1)S(1)} %copy-done), kind=kOutput, calls=%fused_computation.14 | convolution fusion | flops 538181376 | bytes 4723712 | tf_op jit(solution)/shard_map/dot_general | solution.py:69
  45.9 0.0 copy-start.7
  45.9 0.6 convolution_convert_fusion
  46.5 20.6 %all_to_all.24 = bf16[32,16,1024]{2,1,0:T(8,128)(2,1)S(1)} all-to-all(bf16[32,16,1024]{2,1,0:T(8,128)(2,1)S(1)} %bitcast.43), channel_id=1, replica_groups=mesh['graph'=8,'index'=32] {'index'}, dimensions={0} | all-to-all | bytes 2097152 | tf_op jit(solution)/shard_map/all_to_all | solution.py:81
  67.1 0.5 convolution_convert_fusion.3
  67.6 12.7 %all_to_all.25 = bf16[32,16,256]{2,1,0:T(8,128)(2,1)S(1)} all-to-all(bf16[32,16,256]{2,1,0:T(8,128)(2,1)S(1)} %bitcast.47), channel_id=1, replica_groups=mesh['graph'=8,'index'=32] {'index'}, dimensions={0} | all-to-all | bytes 524288 | tf_op jit(solution)/shard_map/all_to_all | solution.py:86
  80.3 0.9 %convolution_convert_fusion.4 = bf16[256,256]{1,0:T(8,128)(2,1)} fusion(bf16[512,256]{1,0:T(8,128)(2,1)S(1)} %bitcast.46, s32[256]{0:T(256)S(1)} %bitcast.51), kind=kOutput, calls=%fused_computation.12 | convolution fusion | flops 67305472 | bytes 394240 | tf_op jit(solution)/shard_map/dot_general | solution.py:93
  (15 shorter events, 0.1 us)
Async XLA Ops:
  0.0 43.8 %copy-start = (bf16[1024,1024]{1,0:T(8,128)(2,1)S(1)}, bf16[1024,1024]{1,0:T(8,128)(2,1)}, u32[]{:S(2)}) copy-start(bf16[1024,1024]{1,0:T(8,128)(2,1)} %param.15) | copy-start | bytes 6291460
  0.0 15.3 %copy-start.1 = (bf16[256,1024]{1,0:T(8,128)(2,1)S(1)}, bf16[256,1024]{1,0:T(8,128)(2,1)}, u32[]{:S(2)}) copy-start(bf16[256,1024]{1,0:T(8,128)(2,1)} %param.11) | copy-start | bytes 1572868
  0.0 15.3 %copy-start.8 = (f32[1024]{0:T(1024)S(1)}, f32[1024]{0:T(1024)}, u32[]{:S(2)}) copy-start(f32[1024]{0:T(1024)} %param.13) | copy-start | bytes 12292
  1.6 15.5 %all-to-all-start = ((f32[32,1,16]{2,1,0:T(1,128)}), f32[32,1,16]{2,1,0:T(1,128)S(1)}, u32[]{:S(2)}, u32[]{:S(2)}) async-start(f32[32,1,16]{2,1,0:T(1,128)} %bitcast.13), calls=%async_computation | async-start | bytes 32768 | tf_op jit(solution)/shard_map/all_to_all | solution.py:41
  11.7 3.6 %copy-start.6 = (bf16[1024,1024]{1,0:T(8,128)(2,1)S(1)}, bf16[1024,1024]{1,0:T(8,128)(2,1)}, u32[]{:S(2)}) copy-start(bf16[1024,1024]{1,0:T(8,128)(2,1)} %param.12) | copy-start | bytes 6291460
  15.3 0.8 copy-start.5
  16.0 10.5 %copy-start.2 = (f32[256,50]{0,1:T(8,128)S(1)}, f32[256,50]{0,1:T(8,128)}, u32[]{:S(2)}) copy-start(f32[256,50]{0,1:T(8,128)} %param.20) | copy-start | bytes 153604
  16.0 10.5 %copy-start.3 = (s32[256,50]{0,1:T(8,128)S(1)}, s32[256,50]{0,1:T(8,128)}, u32[]{:S(2)}) copy-start(s32[256,50]{0,1:T(8,128)} %param.19) | copy-start | bytes 153604
  19.9 24.0 %copy-start.4 = (f32[1024]{0:T(1024)S(1)}, f32[1024]{0:T(1024)}, u32[]{:S(2)}) copy-start(f32[1024]{0:T(1024)} %param.16) | copy-start | bytes 12292
  19.9 23.5 %all-to-all-start.1 = ((bf16[32,16,1024]{2,1,0:T(8,128)(2,1)}), bf16[32,16,1024]{2,1,0:T(8,128)(2,1)S(1)}, u32[]{:S(2)}, u32[]{:S(2)}) async-start(bf16[32,16,1024]{2,1,0:T(8,128)(2,1)} %bitcast.44), calls=%async_computation.1 | async-start | bytes 2097152 | tf_op jit(solution)/shard_map/all_to_all | solution.py:58
  45.9 21.2 %copy-start.7 = (bf16[256,1024]{1,0:T(8,128)(2,1)S(1)}, bf16[256,1024]{1,0:T(8,128)(2,1)}, u32[]{:S(2)}) copy-start(bf16[256,1024]{1,0:T(8,128)(2,1)} %param.17) | copy-start | bytes 1572868
